TPU v7x, 512 devices: a whole 4x4x16 slice. The times are simulated.
512 devices in a mesh: ctx: 64 (over z, y_hi, core), head: 8 (over y_lo, x).
Axes of the slice: x: 4, y: 4 (y_hi: 2, y_lo: 2; y = y_hi * 2 + y_lo), z: 16, core: 2. Of those that a mesh axis runs over, the one named last changes fastest.
Arguments:
- query_states: bfloat16 [32768, 8192], P('ctx', 'head'), may hold values from -5 to 5
- key_states: bfloat16 [32768, 1024], P('ctx', 'head'), may hold values from -5 to 5
- value_states: bfloat16 [32768, 1024], P('ctx', 'head'), may hold values from -6 to 6
- out_grad: bfloat16 [32768, 8192], P('ctx', 'head'), may hold values from -6 to 6
- block_lists: int32 [256, 4], replicated, may hold values from 0 to 255, as said below
Outputs:
- query_grad: bfloat16 [32768, 8192], P(('ctx', 'head'))
- key_grad: bfloat16 [32768, 1024], P(('ctx', 'head'))
- value_grad: bfloat16 [32768, 1024], P(('ctx', 'head'))
Inputs may be any that keep to these rules, and one draw needn't show every extreme that they name: `block_lists`: entry 0 of row b is b. The other entries name distinct blocks below b, each held by the same index of ctx as b or by one of the 8 indices just below it; a row with fewer candidates repeats b in its remaining entries. Taken over the 4 rows of one index of ctx, the listed blocks that another index of ctx holds are at most one distinct block.
All inputs are finite; a program needn't handle non-finite values.
Results may differ from a plain program's by a relative error of at most 0.012.
Values may be sent and summed in bfloat16 or wider, within the bound.
No kernel may reach another device: no remote copies, remote signals or barrier semaphores. Data moves between devices by JAX's collectives and lax.ppermute only.
A program may use at most 64 MiB of HBM per device.

v0:
```python
import math

import jax
import jax.numpy as jnp
from jax import lax
from jax.sharding import PartitionSpec as P

HEADS = 64
KV_HEADS = 8
HEAD_DIM = 128
BLOCK = 128
REACH = 8


def from_behind(x, axis, by):
    devices = lax.axis_size(axis)
    pairs = [(i, i + by) for i in range(devices) if 0 <= i + by < devices]
    return lax.ppermute(x, axis, pairs)


def block_grads(query_blk, grad_blk, kv_blk, entries, block_ids):
    kv_cols = kv_blk.shape[-1] // 2
    kv_heads = kv_cols // HEAD_DIM
    leading = kv_blk.shape[:3]
    scaling = 1.0 / math.sqrt(HEAD_DIM)
    key_blk = kv_blk[..., :kv_cols].reshape(leading + (kv_heads, HEAD_DIM))
    value_blk = kv_blk[..., kv_cols:].reshape(leading + (kv_heads, HEAD_DIM))
    chosen = entries.shape[1]
    order_ids = jnp.arange(chosen, dtype=jnp.int32)
    repeat = (entries[:, :, None] == entries[:, None, :]) & (
        order_ids[None, None, :] < order_ids[None, :, None]
    )
    usable = jnp.logical_not(jnp.any(repeat, axis=2))
    positions = jnp.arange(BLOCK, dtype=jnp.int32)
    causal = positions[None, :] <= positions[:, None]
    earlier = entries < block_ids[:, None]
    allowed = usable[:, None, :, None] & (earlier[:, None, :, None] | causal[None, :, None, :])
    allowed = allowed[:, None, None]
    scores = (
        jnp.einsum("nighd,netgd->nghiet", query_blk, key_blk, preferred_element_type=jnp.float32)
        * scaling
    )
    scores = jnp.where(allowed, scores, -1e30)
    row_max = jnp.max(scores, axis=(4, 5), keepdims=True)
    total = jnp.sum(jnp.where(allowed, jnp.exp(scores - row_max), 0.0), axis=(4, 5), keepdims=True)
    log_total = row_max + jnp.log(total)
    prob = jnp.where(allowed, jnp.exp(scores - log_total), 0.0)
    prob_half = prob.astype(jnp.bfloat16)
    output = jnp.einsum(
        "nghiet,netgd->nighd", prob_half, value_blk, preferred_element_type=jnp.float32
    ).astype(jnp.bfloat16)
    output_wide = lax.optimization_barrier(output).astype(jnp.float32)
    row_dot = jnp.sum(grad_blk.astype(jnp.float32) * output_wide, axis=-1)
    prob_grad = jnp.einsum(
        "nighd,netgd->nghiet", grad_blk, value_blk, preferred_element_type=jnp.float32
    )
    centred = prob_grad - jnp.transpose(row_dot, (0, 2, 3, 1))[..., None, None]
    score_grad = (prob * centred * scaling).astype(jnp.bfloat16)
    block_qgrad = jnp.einsum(
        "nghiet,netgd->nighd", score_grad, key_blk, preferred_element_type=jnp.float32
    ).astype(jnp.bfloat16)
    key_part = jnp.einsum(
        "nghiet,nighd->netgd", score_grad, query_blk, preferred_element_type=jnp.float32
    )
    value_part = jnp.einsum(
        "nghiet,nighd->netgd", prob_half, grad_blk, preferred_element_type=jnp.float32
    )
    pair_terms = jnp.concatenate(
        [key_part.reshape(leading + (kv_cols,)), value_part.reshape(leading + (kv_cols,))], axis=-1
    )
    return (block_qgrad, pair_terms)


def fetch_block(outgoing_one, distance):
    return from_behind(outgoing_one, "ctx", distance)


def return_block(terms_one, distance):
    return from_behind(terms_one.astype(jnp.bfloat16), "ctx", -distance).astype(terms_one.dtype)


def body(query_states, key_states, value_states, out_grad, block_lists):
    ctx_count = lax.axis_size("ctx")
    myself = lax.axis_index("ctx")
    tok_rows = query_states.shape[0]
    kv_cols = key_states.shape[1]
    kv_heads = kv_cols // HEAD_DIM
    group_size = HEADS // KV_HEADS
    blocks_here = tok_rows // BLOCK
    chosen = block_lists.shape[1]
    lists_by_dev = block_lists.reshape(ctx_count, blocks_here * chosen)
    slot_ids = jnp.arange(blocks_here, dtype=jnp.int32)
    distances = jnp.arange(1, REACH + 1, dtype=jnp.int32)
    targets = myself + distances
    target_ok = targets < ctx_count
    target_rows = jnp.take(lists_by_dev, jnp.minimum(targets, ctx_count - 1), axis=0)
    mine = target_rows // blocks_here == myself
    requested = jnp.max(jnp.where(mine, target_rows % blocks_here, -1), axis=1)
    requested = jnp.where(target_ok, requested, -1)
    kv_local = jnp.concatenate([key_states, value_states], axis=1).reshape(
        blocks_here, BLOCK, 2 * kv_cols
    )
    pick_rows = (requested[:, None] == slot_ids[None, :]).astype(jnp.bfloat16)
    outgoing = jnp.einsum(
        "sj,jtc->stc", pick_rows, kv_local, preferred_element_type=jnp.float32
    ).astype(jnp.bfloat16)
    arrivals = []
    for distance in range(1, REACH + 1):
        arrivals.append(fetch_block(outgoing[distance - 1], distance))
    incoming = jnp.stack(arrivals, axis=0)
    own_entries = lax.dynamic_slice_in_dim(block_lists, myself * blocks_here, blocks_here, 0)
    flat_entries = own_entries.reshape(blocks_here * chosen)
    behind = myself - flat_entries // blocks_here
    at_home = behind == 0
    source_row = jnp.where(at_home, REACH + flat_entries % blocks_here, behind - 1)
    kv_stock = jnp.concatenate([incoming, kv_local], axis=0)
    gathered = jnp.take(kv_stock, source_row, axis=0).reshape(
        blocks_here, chosen, BLOCK, 2 * kv_cols
    )
    per_step = 1
    step_count = blocks_here // per_step
    query_steps = query_states.reshape(step_count, per_step, BLOCK, kv_heads, group_size, HEAD_DIM)
    grad_steps = out_grad.reshape(step_count, per_step, BLOCK, kv_heads, group_size, HEAD_DIM)
    kv_steps = gathered.reshape(step_count, per_step, chosen, BLOCK, 2 * kv_cols)
    entry_steps = own_entries.reshape(step_count, per_step, chosen)
    block_steps = (myself * blocks_here + slot_ids).reshape(step_count, per_step)

    def one_step(pieces):
        return block_grads(pieces[0], pieces[1], pieces[2], pieces[3], pieces[4])

    qgrad_steps, pair_steps = lax.map(
        one_step, (query_steps, grad_steps, kv_steps, entry_steps, block_steps)
    )
    query_local = qgrad_steps.reshape(tok_rows, kv_heads * group_size * HEAD_DIM)
    pair_terms = pair_steps.reshape(blocks_here * chosen, BLOCK, 2 * kv_cols)
    keep_home = (
        at_home[None, :] & ((flat_entries % blocks_here)[None, :] == slot_ids[:, None])
    ).astype(jnp.float32)
    totals = jnp.einsum("jp,ptc->jtc", keep_home, pair_terms, precision=lax.Precision.HIGHEST)
    by_distance = behind[None, :] == distances[:, None]
    sendback = jnp.einsum(
        "sp,ptc->stc", by_distance.astype(jnp.float32), pair_terms, precision=lax.Precision.HIGHEST
    )
    returned = []
    for distance in range(1, REACH + 1):
        returned.append(return_block(sendback[distance - 1], distance))
    arrived = jnp.stack(returned, axis=0)
    credit = (requested[None, :] == slot_ids[:, None]).astype(jnp.float32)
    totals = totals + jnp.einsum("js,stc->jtc", credit, arrived, precision=lax.Precision.HIGHEST)
    key_local = totals[..., :kv_cols].reshape(tok_rows, kv_cols).astype(jnp.bfloat16)
    value_local = totals[..., kv_cols:].reshape(tok_rows, kv_cols).astype(jnp.bfloat16)
    query_grad, key_grad, value_grad = (
        lax.all_to_all(query_local, "head", split_axis=0, concat_axis=1, tiled=True),
        lax.all_to_all(key_local, "head", split_axis=0, concat_axis=1, tiled=True),
        lax.all_to_all(value_local, "head", split_axis=0, concat_axis=1, tiled=True),
    )
    return (query_grad, key_grad, value_grad)


def solution(mesh):
    in_specs = (P("ctx", "head"), P("ctx", "head"), P("ctx", "head"), P("ctx", "head"), P())
    out_specs = (P(("ctx", "head"), None), P(("ctx", "head"), None), P(("ctx", "head"), None))
    return jax.shard_map(body, mesh=mesh, in_specs=in_specs, out_specs=out_specs, check_vma=False)
```

profile of v0, /device:TPU:64, one launch (start us, length us, event | category | flops | bytes accessed | tf_op | source)
XLA Modules:
  0.0 164.2 jit_solution(14954413630219802681)
XLA Ops:
  2.4 1.0 pad_maximum_fusion
  3.8 0.9 fusion.55
  5.4 1.9 %collective-permute-start = (bf16[128,256]{1,0:T(8,128)(2,1)}, bf16[128,256]{1,0:T(8,128)(2,1)}, u32[]{:S(2)}, u32[]{:S(2)}) collective-permute-start(bf16[128,256]{1,0:T(8,128)(2,1)} %bitcast.256), channel_id=1, source_target_pairs={{0,8},{8,16},{16,24},{24,32},{32,40},{40,48},{48,56},{56,64},{64,7... | collective-permute-start | bytes 196616 | tf_op jit(solution)/shard_map/ppermute | solution.py:18
  7.9 5.1 %collective-permute-start.1 = (bf16[128,256]{1,0:T(8,128)(2,1)}, bf16[128,256]{1,0:T(8,128)(2,1)}, u32[]{:S(2)}, u32[]{:S(2)}) collective-permute-start(bf16[128,256]{1,0:T(8,128)(2,1)} %bitcast.255), channel_id=1, source_target_pairs={{0,16},{8,24},{16,32},{24,40},{32,48},{40,56},{48,64},{56,72},{64,... | collective-permute-start | bytes 196616 | tf_op jit(solution)/shard_map/ppermute | solution.py:18
  13.7 6.2 %collective-permute-start.2 = (bf16[128,256]{1,0:T(8,128)(2,1)}, bf16[128,256]{1,0:T(8,128)(2,1)}, u32[]{:S(2)}, u32[]{:S(2)}) collective-permute-start(bf16[128,256]{1,0:T(8,128)(2,1)} %bitcast.254), channel_id=1, source_target_pairs={{0,24},{8,32},{16,40},{24,48},{32,56},{40,64},{48,72},{56,80},{64,... | collective-permute-start | bytes 196616 | tf_op jit(solution)/shard_map/ppermute | solution.py:18
  19.9 5.0 %collective-permute-start.3 = (bf16[128,256]{1,0:T(8,128)(2,1)S(1)}, bf16[128,256]{1,0:T(8,128)(2,1)}, u32[]{:S(2)}, u32[]{:S(2)}) collective-permute-start(bf16[128,256]{1,0:T(8,128)(2,1)S(1)} %bitcast.319), channel_id=1, source_target_pairs={{0,32},{8,40},{16,48},{24,56},{32,64},{40,72},{48,80},{56,88},{64,... | collective-permute-start | bytes 196616 | tf_op jit(solution)/shard_map/ppermute | solution.py:18
  25.0 1.9 %collective-permute-start.4 = (bf16[128,256]{1,0:T(8,128)(2,1)S(1)}, bf16[128,256]{1,0:T(8,128)(2,1)}, u32[]{:S(2)}, u32[]{:S(2)}) collective-permute-start(bf16[128,256]{1,0:T(8,128)(2,1)S(1)} %bitcast.318), channel_id=1, source_target_pairs={{0,40},{8,48},{16,56},{24,64},{32,72},{40,80},{48,88},{56,96},{64,... | collective-permute-start | bytes 196616 | tf_op jit(solution)/shard_map/ppermute | solution.py:18
  29.0 1.3 copy.400
  30.8 4.9 %collective-permute-start.5 = (bf16[128,256]{1,0:T(8,128)(2,1)S(1)}, bf16[128,256]{1,0:T(8,128)(2,1)S(1)}, u32[]{:S(2)}, u32[]{:S(2)}) collective-permute-start(bf16[128,256]{1,0:T(8,128)(2,1)S(1)} %bitcast.330), channel_id=1, source_target_pairs={{0,48},{8,56},{16,64},{24,72},{32,80},{40,88},{48,96},{56,104},{64... | collective-permute-start | bytes 196616 | tf_op jit(solution)/shard_map/ppermute | solution.py:18
  35.8 0.8 bitcast_dynamic-update-slice_fusion.7
  36.6 9.2 %collective-permute-start.6 = (bf16[128,256]{1,0:T(8,128)(2,1)S(1)}, bf16[128,256]{1,0:T(8,128)(2,1)S(1)}, u32[]{:S(2)}, u32[]{:S(2)}) collective-permute-start(bf16[128,256]{1,0:T(8,128)(2,1)S(1)} %bitcast.324), channel_id=1, source_target_pairs={{0,56},{8,64},{16,72},{24,80},{32,88},{40,96},{48,104},{56,112},{6... | collective-permute-start | bytes 196616 | tf_op jit(solution)/shard_map/ppermute | solution.py:18
  45.8 0.8 bitcast_dynamic-update-slice_fusion.6
  46.7 3.4 %collective-permute-start.7 = (bf16[128,256]{1,0:T(8,128)(2,1)S(1)}, bf16[128,256]{1,0:T(8,128)(2,1)S(1)}, u32[]{:S(2)}, u32[]{:S(2)}) collective-permute-start(bf16[128,256]{1,0:T(8,128)(2,1)S(1)} %bitcast.321), channel_id=1, source_target_pairs={{0,64},{8,72},{16,80},{24,88},{32,96},{40,104},{48,112},{56,120},{... | collective-permute-start | bytes 196616 | tf_op jit(solution)/shard_map/ppermute | solution.py:18
  50.1 0.8 bitcast_dynamic-update-slice_fusion.5
  50.9 0.8 bitcast_dynamic-update-slice_fusion.4
  51.8 0.8 bitcast_dynamic-update-slice_fusion.3
  52.7 1.2 collective-permute-done.7
  54.7 32.7 %while.12 = (s32[]{:T(128)}, bf16[4,1,128,1,8,128]{5,4,2,0,3,1:T(8,128)(2,1)}, f32[4,1,4,128,256]{3,4,2,1,0:T(8,128)}, bf16[4,1,4,128,256]{4,3,2,1,0:T(8,128)(2,...) while((s32[]{:T(128)}, ...), condition=%wide.region_6.7_spmd, body=%wide.region_1.6_spmd.sunk | while | flops 815806528 | bytes 21442768 | solution.py:131
  56.3 1.0 constant_dynamic-slice_fusion.8
  62.0 0.9 fusion.87
  64.5 1.0 constant_dynamic-slice_fusion.8
  70.2 0.8 fusion.87
  72.7 1.0 constant_dynamic-slice_fusion.8
  78.4 0.8 fusion.87
  80.8 1.0 constant_dynamic-slice_fusion.8
  87.4 2.2 %copy.339 = f32[16,128,256]{2,0,1:T(8,128)S(1)} copy(f32[16,128,256]{1,2,0:T(8,128)} %bitcast.313) | data formatting | bytes 4194304 | tf_op jit(solution)/shard_map/reshape | solution.py:135
  90.5 0.9 fusion.54
  91.5 1.9 %collective-permute-start.8 = (bf16[128,256]{1,0:T(8,128)(2,1)S(1)}, bf16[128,256]{1,0:T(8,128)(2,1)S(1)}, u32[]{:S(2)}, u32[]{:S(2)}) collective-permute-start(bf16[128,256]{1,0:T(8,128)(2,1)S(1)} %bitcast.338), channel_id=1, source_target_pairs={{8,0},{16,8},{24,16},{32,24},{40,32},{48,40},{56,48},{64,56},{72,6... | collective-permute-start | bytes 196616 | tf_op jit(solution)/shard_map/ppermute | solution.py:18
  93.4 4.4 %collective-permute-start.9 = (bf16[128,256]{1,0:T(8,128)(2,1)S(1)}, bf16[128,256]{1,0:T(8,128)(2,1)S(1)}, u32[]{:S(2)}, u32[]{:S(2)}) collective-permute-start(bf16[128,256]{1,0:T(8,128)(2,1)S(1)} %bitcast.332), channel_id=1, source_target_pairs={{16,0},{24,8},{32,16},{40,24},{48,32},{56,40},{64,48},{72,56},{80,... | collective-permute-start | bytes 196616 | tf_op jit(solution)/shard_map/ppermute | solution.py:18
  97.8 2.7 %collective-permute-start.10 = (bf16[128,256]{1,0:T(8,128)(2,1)S(1)}, bf16[128,256]{1,0:T(8,128)(2,1)S(1)}, u32[]{:S(2)}, u32[]{:S(2)}) collective-permute-start(bf16[128,256]{1,0:T(8,128)(2,1)S(1)} %bitcast.328), channel_id=1, source_target_pairs={{24,0},{32,8},{40,16},{48,24},{56,32},{64,40},{72,48},{80,56},{88,... | collective-permute-start | bytes 196616 | tf_op jit(solution)/shard_map/ppermute | solution.py:18
  100.7 2.1 %collective-permute-start.11 = (bf16[128,256]{1,0:T(8,128)(2,1)S(1)}, bf16[128,256]{1,0:T(8,128)(2,1)S(1)}, u32[]{:S(2)}, u32[]{:S(2)}) collective-permute-start(bf16[128,256]{1,0:T(8,128)(2,1)S(1)} %bitcast.333), channel_id=1, source_target_pairs={{32,0},{40,8},{48,16},{56,24},{64,32},{72,40},{80,48},{88,56},{96,... | collective-permute-start | bytes 196616 | tf_op jit(solution)/shard_map/ppermute | solution.py:18
  102.8 1.9 %collective-permute-start.12 = (bf16[128,256]{1,0:T(8,128)(2,1)S(1)}, bf16[128,256]{1,0:T(8,128)(2,1)S(1)}, u32[]{:S(2)}, u32[]{:S(2)}) collective-permute-start(bf16[128,256]{1,0:T(8,128)(2,1)S(1)} %bitcast.329), channel_id=1, source_target_pairs={{40,0},{48,8},{56,16},{64,24},{72,32},{80,40},{88,48},{96,56},{104... | collective-permute-start | bytes 196616 | tf_op jit(solution)/shard_map/ppermute | solution.py:18
  104.7 1.9 %collective-permute-start.13 = (bf16[128,256]{1,0:T(8,128)(2,1)S(1)}, bf16[128,256]{1,0:T(8,128)(2,1)S(1)}, u32[]{:S(2)}, u32[]{:S(2)}) collective-permute-start(bf16[128,256]{1,0:T(8,128)(2,1)S(1)} %bitcast.323), channel_id=1, source_target_pairs={{48,0},{56,8},{64,16},{72,24},{80,32},{88,40},{96,48},{104,56},{11... | collective-permute-start | bytes 196616 | tf_op jit(solution)/shard_map/ppermute | solution.py:18
  106.7 1.9 %collective-permute-start.14 = (bf16[128,256]{1,0:T(8,128)(2,1)S(1)}, bf16[128,256]{1,0:T(8,128)(2,1)S(1)}, u32[]{:S(2)}, u32[]{:S(2)}) collective-permute-start(bf16[128,256]{1,0:T(8,128)(2,1)S(1)} %bitcast.322), channel_id=1, source_target_pairs={{56,0},{64,8},{72,16},{80,24},{88,32},{96,40},{104,48},{112,56},{1... | collective-permute-start | bytes 196616 | tf_op jit(solution)/shard_map/ppermute | solution.py:18
  108.6 2.1 %collective-permute-start.15 = (bf16[128,256]{1,0:T(8,128)(2,1)S(1)}, bf16[128,256]{1,0:T(8,128)(2,1)S(1)}, u32[]{:S(2)}, u32[]{:S(2)}) collective-permute-start(bf16[128,256]{1,0:T(8,128)(2,1)S(1)} %bitcast.320), channel_id=1, source_target_pairs={{64,0},{72,8},{80,16},{88,24},{96,32},{104,40},{112,48},{120,56},{... | collective-permute-start | bytes 196616 | tf_op jit(solution)/shard_map/ppermute | solution.py:18
  110.7 0.8 fusion.39
  112.1 1.1 collective-permute-done.13
  113.4 1.4 collective-permute-done.14
  114.9 7.6 %collective-permute-done.15 = bf16[128,256]{1,0:T(8,128)(2,1)S(1)} collective-permute-done((bf16[128,256]{1,0:T(8,128)(2,1)S(1)}, bf16[128,256]{1,0:T(8,128)(2,1)S(1)}, u32[]{:S(2)}, u32[]{:S(2)}) %collective-permute-start.15) | collective-permute-done | bytes 65568 | tf_op jit(solution)/shard_map/ppermute | solution.py:18
  122.6 1.6 stack.78
  125.3 4.4 %all-to-all-start.2 = ((bf16[8,64,128]{2,1,0:T(8,128)(2,1)}), bf16[8,64,128]{2,1,0:T(8,128)(2,1)S(1)}, u32[]{:S(2)}, u32[]{:S(2)}) async-start(bf16[8,64,128]{2,1,0:T(8,128)(2,1)} %bitcast.78), calls=%async_computation.2 | async-start | bytes 262144 | tf_op jit(solution)/shard_map/all_to_all | solution.py:155
  130.4 5.9 %all-to-all-done.2 = bf16[8,64,128]{2,1,0:T(8,128)(2,1)S(1)} async-done(((bf16[8,64,128]{2,1,0:T(8,128)(2,1)}), bf16[8,64,128]{2,1,0:T(8,128)(2,1)S(1)}, u32[]{:S(2)}, u32[]{:S(2)}) %all-to-all-start.2) | async-done | bytes 131104 | tf_op jit(solution)/shard_map/all_to_all | solution.py:155
  136.3 3.4 %all-to-all-start.1 = ((bf16[8,64,128]{2,1,0:T(8,128)(2,1)}), bf16[8,64,128]{2,1,0:T(8,128)(2,1)S(1)}, u32[]{:S(2)}, u32[]{:S(2)}) async-start(bf16[8,64,128]{2,1,0:T(8,128)(2,1)} %bitcast.76), calls=%async_computation.1 | async-start | bytes 262144 | tf_op jit(solution)/shard_map/all_to_all | solution.py:154
  139.7 1.3 all_to_all.38
  140.9 5.2 %all-to-all-done.1 = bf16[8,64,128]{2,1,0:T(8,128)(2,1)S(1)} async-done(((bf16[8,64,128]{2,1,0:T(8,128)(2,1)}), bf16[8,64,128]{2,1,0:T(8,128)(2,1)S(1)}, u32[]{:S(2)}, u32[]{:S(2)}) %all-to-all-start.1) | async-done | bytes 131104 | tf_op jit(solution)/shard_map/all_to_all | solution.py:154
  146.2 3.6 %all-to-all-start = ((bf16[8,64,1024]{2,1,0:T(8,128)(2,1)}), bf16[8,64,1024]{2,1,0:T(8,128)(2,1)S(1)}, u32[]{:S(2)}, u32[]{:S(2)}) async-start(bf16[8,64,1024]{2,1,0:T(8,128)(2,1)} %all_to_all.38), calls=%async_computation | async-start | bytes 2097152 | tf_op jit(solution)/shard_map/all_to_all | solution.py:153
  151.1 12.1 %all-to-all-done = bf16[8,64,1024]{2,1,0:T(8,128)(2,1)S(1)} async-done(((bf16[8,64,1024]{2,1,0:T(8,128)(2,1)}), bf16[8,64,1024]{2,1,0:T(8,128)(2,1)S(1)}, u32[]{:S(2)}, u32[]{:S(2)}) %all-to-all-start) | async-done | bytes 1048608 | tf_op jit(solution)/shard_map/all_to_all | solution.py:153
  163.2 1.1 copy.396
  (172 shorter events, 38.0 us)
Async XLA Ops:
  2.4 1.4 copy-start.6
  2.4 25.1 %copy-start.3 = (s32[256,4]{0,1:T(4,128)S(1)}, s32[256,4]{0,1:T(4,128)}, u32[]{:S(2)}) copy-start(s32[256,4]{0,1:T(4,128)} %param.11) | copy-start | bytes 12292
  3.4 25.3 %copy-start = (bf16[512,1024]{1,0:T(8,128)(2,1)S(1)}, bf16[512,1024]{1,0:T(8,128)(2,1)}, u32[]{:S(2)}) copy-start(bf16[512,1024]{1,0:T(8,128)(2,1)} %param.7) | copy-start | bytes 3145732
  4.7 24.2 %copy-start.1 = (bf16[512,1024]{1,0:T(8,128)(2,1)S(1)}, bf16[512,1024]{1,0:T(8,128)(2,1)}, u32[]{:S(2)}) copy-start(bf16[512,1024]{1,0:T(8,128)(2,1)} %param.10) | copy-start | bytes 3145732
  5.4 25.4 %collective-permute-start = (bf16[128,256]{1,0:T(8,128)(2,1)}, bf16[128,256]{1,0:T(8,128)(2,1)}, u32[]{:S(2)}, u32[]{:S(2)}) collective-permute-start(bf16[128,256]{1,0:T(8,128)(2,1)} %bitcast.256), channel_id=1, source_target_pairs={{0,8},{8,16},{16,24},{24,32},{32,40},{40,48},{48,56},{56,64},{64,7... | collective-permute-start | bytes 196616 | tf_op jit(solution)/shard_map/ppermute | solution.py:18
  7.9 28.7 %collective-permute-start.1 = (bf16[128,256]{1,0:T(8,128)(2,1)}, bf16[128,256]{1,0:T(8,128)(2,1)}, u32[]{:S(2)}, u32[]{:S(2)}) collective-permute-start(bf16[128,256]{1,0:T(8,128)(2,1)} %bitcast.255), channel_id=1, source_target_pairs={{0,16},{8,24},{16,32},{24,40},{32,48},{40,56},{48,64},{56,72},{64,... | collective-permute-start | bytes 196616 | tf_op jit(solution)/shard_map/ppermute | solution.py:18
  13.7 33.0 %collective-permute-start.2 = (bf16[128,256]{1,0:T(8,128)(2,1)}, bf16[128,256]{1,0:T(8,128)(2,1)}, u32[]{:S(2)}, u32[]{:S(2)}) collective-permute-start(bf16[128,256]{1,0:T(8,128)(2,1)} %bitcast.254), channel_id=1, source_target_pairs={{0,24},{8,32},{16,40},{24,48},{32,56},{40,64},{48,72},{56,80},{64,... | collective-permute-start | bytes 196616 | tf_op jit(solution)/shard_map/ppermute | solution.py:18
  19.9 31.0 %collective-permute-start.3 = (bf16[128,256]{1,0:T(8,128)(2,1)S(1)}, bf16[128,256]{1,0:T(8,128)(2,1)}, u32[]{:S(2)}, u32[]{:S(2)}) collective-permute-start(bf16[128,256]{1,0:T(8,128)(2,1)S(1)} %bitcast.319), channel_id=1, source_target_pairs={{0,32},{8,40},{16,48},{24,56},{32,64},{40,72},{48,80},{56,88},{64,... | collective-permute-start | bytes 196616 | tf_op jit(solution)/shard_map/ppermute | solution.py:18
  25.0 26.8 %collective-permute-start.4 = (bf16[128,256]{1,0:T(8,128)(2,1)S(1)}, bf16[128,256]{1,0:T(8,128)(2,1)}, u32[]{:S(2)}, u32[]{:S(2)}) collective-permute-start(bf16[128,256]{1,0:T(8,128)(2,1)S(1)} %bitcast.318), channel_id=1, source_target_pairs={{0,40},{8,48},{16,56},{24,64},{32,72},{40,80},{48,88},{56,96},{64,... | collective-permute-start | bytes 196616 | tf_op jit(solution)/shard_map/ppermute | solution.py:18
  27.7 0.8 copy-start.4
  30.2 24.3 %copy-start.9 = (pred[4,4]{1,0:T(4,128)(4,1)S(1)}, pred[4,4]{1,0:T(4,128)(4,1)}, u32[]{:S(2)}) copy-start(pred[4,4]{1,0:T(4,128)(4,1)} %copy.327) | copy-start | bytes 52
  30.8 21.8 %collective-permute-start.5 = (bf16[128,256]{1,0:T(8,128)(2,1)S(1)}, bf16[128,256]{1,0:T(8,128)(2,1)S(1)}, u32[]{:S(2)}, u32[]{:S(2)}) collective-permute-start(bf16[128,256]{1,0:T(8,128)(2,1)S(1)} %bitcast.330), channel_id=1, source_target_pairs={{0,48},{8,56},{16,64},{24,72},{32,80},{40,88},{48,96},{56,104},{64... | collective-permute-start | bytes 196616 | tf_op jit(solution)/shard_map/ppermute | solution.py:18
  36.6 16.0 %collective-permute-start.6 = (bf16[128,256]{1,0:T(8,128)(2,1)S(1)}, bf16[128,256]{1,0:T(8,128)(2,1)S(1)}, u32[]{:S(2)}, u32[]{:S(2)}) collective-permute-start(bf16[128,256]{1,0:T(8,128)(2,1)S(1)} %bitcast.324), channel_id=1, source_target_pairs={{0,56},{8,64},{16,72},{24,80},{32,88},{40,96},{48,104},{56,112},{6... | collective-permute-start | bytes 196616 | tf_op jit(solution)/shard_map/ppermute | solution.py:18
  46.7 7.1 %collective-permute-start.7 = (bf16[128,256]{1,0:T(8,128)(2,1)S(1)}, bf16[128,256]{1,0:T(8,128)(2,1)S(1)}, u32[]{:S(2)}, u32[]{:S(2)}) collective-permute-start(bf16[128,256]{1,0:T(8,128)(2,1)S(1)} %bitcast.321), channel_id=1, source_target_pairs={{0,64},{8,72},{16,80},{24,88},{32,96},{40,104},{48,112},{56,120},{... | collective-permute-start | bytes 196616 | tf_op jit(solution)/shard_map/ppermute | solution.py:18
  53.9 0.8 copy-start.10
  87.4 2.2 %copy-start.8 = (s32[8]{0:T(128)S(1)}, s32[8]{0:T(128)}, u32[]{:S(2)}) copy-start(s32[8]{0:T(128)} %iota_add_fusion.1) | copy-start | bytes 100
  89.7 10.9 %copy-start.5 = (s32[16]{0:T(128)S(1)}, s32[16]{0:T(128)}, u32[]{:S(2)}) copy-start(s32[16]{0:T(128)} %copy-done.4) | copy-start | bytes 196
  91.5 13.2 %collective-permute-start.8 = (bf16[128,256]{1,0:T(8,128)(2,1)S(1)}, bf16[128,256]{1,0:T(8,128)(2,1)S(1)}, u32[]{:S(2)}, u32[]{:S(2)}) collective-permute-start(bf16[128,256]{1,0:T(8,128)(2,1)S(1)} %bitcast.338), channel_id=1, source_target_pairs={{8,0},{16,8},{24,16},{32,24},{40,32},{48,40},{56,48},{64,56},{72,6... | collective-permute-start | bytes 196616 | tf_op jit(solution)/shard_map/ppermute | solution.py:18
  93.4 13.2 %collective-permute-start.9 = (bf16[128,256]{1,0:T(8,128)(2,1)S(1)}, bf16[128,256]{1,0:T(8,128)(2,1)S(1)}, u32[]{:S(2)}, u32[]{:S(2)}) collective-permute-start(bf16[128,256]{1,0:T(8,128)(2,1)S(1)} %bitcast.332), channel_id=1, source_target_pairs={{16,0},{24,8},{32,16},{40,24},{48,32},{56,40},{64,48},{72,56},{80,... | collective-permute-start | bytes 196616 | tf_op jit(solution)/shard_map/ppermute | solution.py:18
  97.8 10.8 %collective-permute-start.10 = (bf16[128,256]{1,0:T(8,128)(2,1)S(1)}, bf16[128,256]{1,0:T(8,128)(2,1)S(1)}, u32[]{:S(2)}, u32[]{:S(2)}) collective-permute-start(bf16[128,256]{1,0:T(8,128)(2,1)S(1)} %bitcast.328), channel_id=1, source_target_pairs={{24,0},{32,8},{40,16},{48,24},{56,32},{64,40},{72,48},{80,56},{88,... | collective-permute-start | bytes 196616 | tf_op jit(solution)/shard_map/ppermute | solution.py:18
  100.7 11.2 %collective-permute-start.11 = (bf16[128,256]{1,0:T(8,128)(2,1)S(1)}, bf16[128,256]{1,0:T(8,128)(2,1)S(1)}, u32[]{:S(2)}, u32[]{:S(2)}) collective-permute-start(bf16[128,256]{1,0:T(8,128)(2,1)S(1)} %bitcast.333), channel_id=1, source_target_pairs={{32,0},{40,8},{48,16},{56,24},{64,32},{72,40},{80,48},{88,56},{96,... | collective-permute-start | bytes 196616 | tf_op jit(solution)/shard_map/ppermute | solution.py:18
  102.8 9.2 %collective-permute-start.12 = (bf16[128,256]{1,0:T(8,128)(2,1)S(1)}, bf16[128,256]{1,0:T(8,128)(2,1)S(1)}, u32[]{:S(2)}, u32[]{:S(2)}) collective-permute-start(bf16[128,256]{1,0:T(8,128)(2,1)S(1)} %bitcast.329), channel_id=1, source_target_pairs={{40,0},{48,8},{56,16},{64,24},{72,32},{80,40},{88,48},{96,56},{104... | collective-permute-start | bytes 196616 | tf_op jit(solution)/shard_map/ppermute | solution.py:18
  104.7 8.6 %collective-permute-start.13 = (bf16[128,256]{1,0:T(8,128)(2,1)S(1)}, bf16[128,256]{1,0:T(8,128)(2,1)S(1)}, u32[]{:S(2)}, u32[]{:S(2)}) collective-permute-start(bf16[128,256]{1,0:T(8,128)(2,1)S(1)} %bitcast.323), channel_id=1, source_target_pairs={{48,0},{56,8},{64,16},{72,24},{80,32},{88,40},{96,48},{104,56},{11... | collective-permute-start | bytes 196616 | tf_op jit(solution)/shard_map/ppermute | solution.py:18
  106.7 8.1 %collective-permute-start.14 = (bf16[128,256]{1,0:T(8,128)(2,1)S(1)}, bf16[128,256]{1,0:T(8,128)(2,1)S(1)}, u32[]{:S(2)}, u32[]{:S(2)}) collective-permute-start(bf16[128,256]{1,0:T(8,128)(2,1)S(1)} %bitcast.322), channel_id=1, source_target_pairs={{56,0},{64,8},{72,16},{80,24},{88,32},{96,40},{104,48},{112,56},{1... | collective-permute-start | bytes 196616 | tf_op jit(solution)/shard_map/ppermute | solution.py:18
  108.6 13.9 %collective-permute-start.15 = (bf16[128,256]{1,0:T(8,128)(2,1)S(1)}, bf16[128,256]{1,0:T(8,128)(2,1)S(1)}, u32[]{:S(2)}, u32[]{:S(2)}) collective-permute-start(bf16[128,256]{1,0:T(8,128)(2,1)S(1)} %bitcast.320), channel_id=1, source_target_pairs={{64,0},{72,8},{80,16},{88,24},{96,32},{104,40},{112,48},{120,56},{... | collective-permute-start | bytes 196616 | tf_op jit(solution)/shard_map/ppermute | solution.py:18
  111.6 12.7 %copy-start.7 = (s32[8]{0:T(128)S(1)}, s32[8]{0:T(128)}, u32[]{:S(2)}) copy-start(s32[8]{0:T(128)} %copy-done.6) | copy-start | bytes 100
  122.6 17.0 %copy-start.2 = (bf16[4,1,128,1,8,128]{5,4,2,0,3,1:T(8,128)(2,1)S(1)}, bf16[4,1,128,1,8,128]{5,4,2,0,3,1:T(8,128)(2,1)}, u32[]{:S(2)}) copy-start(bf16[4,1,128,1,8,128]{5,4,2,0,3,1:T(8,128)(2,1)} %get-tuple-element.46) | copy-start | bytes 3145732
  125.3 11.0 %all-to-all-start.2 = ((bf16[8,64,128]{2,1,0:T(8,128)(2,1)}), bf16[8,64,128]{2,1,0:T(8,128)(2,1)S(1)}, u32[]{:S(2)}, u32[]{:S(2)}) async-start(bf16[8,64,128]{2,1,0:T(8,128)(2,1)} %bitcast.78), calls=%async_computation.2 | async-start | bytes 262144 | tf_op jit(solution)/shard_map/all_to_all | solution.py:155
  136.3 9.9 %all-to-all-start.1 = ((bf16[8,64,128]{2,1,0:T(8,128)(2,1)}), bf16[8,64,128]{2,1,0:T(8,128)(2,1)S(1)}, u32[]{:S(2)}, u32[]{:S(2)}) async-start(bf16[8,64,128]{2,1,0:T(8,128)(2,1)} %bitcast.76), calls=%async_computation.1 | async-start | bytes 262144 | tf_op jit(solution)/shard_map/all_to_all | solution.py:154
  146.2 17.0 %all-to-all-start = ((bf16[8,64,1024]{2,1,0:T(8,128)(2,1)}), bf16[8,64,1024]{2,1,0:T(8,128)(2,1)S(1)}, u32[]{:S(2)}, u32[]{:S(2)}) async-start(bf16[8,64,1024]{2,1,0:T(8,128)(2,1)} %all_to_all.38), calls=%async_computation | async-start | bytes 2097152 | tf_op jit(solution)/shard_map/all_to_all | solution.py:153
where the time goes:
time: 165 us; the launch traced here: 164 us
  starting transfers between devices  68 us (41%)
  waiting for transfers between devices  34.6 us (21%)
  local copies, waits for them, and re-layouts  33.6 us (20%)
  matrix products  14.5 us (9%)
  other arithmetic  11.8 us (7%)
    ppermute x16, starting transfers between devices, from_behind(): return lax.ppermute(x, axis, pairs)  56.7 us
    all_to_all x1, waiting for transfers between devices, body(): lax.all_to_all(query_local, 'head', split_axis=0, concat_axis=1, tiled=True)  12.1 us
    ppermute x16, waiting for transfers between devices, from_behind(): return lax.ppermute(x, axis, pairs)  11.4 us
    unnamed x49, local copies, waits for them, and re-layouts  8.68 us
    dynamic_slice x12, local copies, waits for them, and re-layouts, body(): lax.map(one_step, (query_steps, grad_steps, kv_steps, entry_steps, block_...  7.2 us
    all_to_all x1, waiting for transfers between devices, body(): lax.all_to_all(value_local, 'head', split_axis=0, concat_axis=1, tiled=True)  5.91 us
    all_to_all x1, waiting for transfers between devices, body(): lax.all_to_all(key_local, 'head', split_axis=0, concat_axis=1, tiled=True)  5.24 us
    all_to_all x1, starting transfers between devices, body(): lax.all_to_all(value_local, 'head', split_axis=0, concat_axis=1, tiled=True)  4.37 us
  transfers between devices with their start and end apart: 19, of which 7 were waited for; matrix products, arithmetic and copies ran while one was open for 8% of the time, Pallas kernels for 0%

commit v1 on v0

v1 whole, which is shorter than its diff:
```python
import functools
import math

import jax
import jax.numpy as jnp
from jax import lax
from jax.experimental import pallas as pl
from jax.experimental.pallas import tpu as pltpu
from jax.sharding import PartitionSpec as P

HEADS = 64
KV_HEADS = 8
HEAD_DIM = 128
BLOCK = 128
REACH = 8


def from_behind(x, axis, by):
    devices = lax.axis_size(axis)
    pairs = [(i, i + by) for i in range(devices) if 0 <= i + by < devices]
    return lax.ppermute(x, axis, pairs)


def attn_kernel(slot_ref, use_ref, early_ref, q_ref, g_ref, kv_ref, dq_ref, acc_ref, kv_scr, dk_scr, dv_scr,
                *, chosen, group, scaling):
    n = pl.program_id(0)

    @pl.when(n == 0)
    def _():
        acc_ref[...] = jnp.zeros_like(acc_ref)

    keys = chosen * BLOCK
    for e in range(chosen):
        kv_scr[e * BLOCK:(e + 1) * BLOCK, :] = kv_ref[slot_ref[n * chosen + e]]
    key_cat = kv_scr[:, :HEAD_DIM]
    value_cat = kv_scr[:, HEAD_DIM:]

    col = lax.broadcasted_iota(jnp.int32, (BLOCK, keys), 1)
    row = lax.broadcasted_iota(jnp.int32, (BLOCK, keys), 0)
    ent = col // BLOCK
    tok = col % BLOCK
    use_col = jnp.zeros((BLOCK, keys), jnp.int32)
    early_col = jnp.zeros((BLOCK, keys), jnp.int32)
    for e in range(chosen):
        use_col = jnp.where(ent == e, use_ref[n * chosen + e], use_col)
        early_col = jnp.where(ent == e, early_ref[n * chosen + e], early_col)
    allowed = (use_col != 0) & ((early_col != 0) | (tok <= row))

    dk_scr[...] = jnp.zeros_like(dk_scr)
    dv_scr[...] = jnp.zeros_like(dv_scr)
    nt = (((1,), (1,)), ((), ()))
    tn = (((0,), (0,)), ((), ()))
    for h in range(group):
        cols = slice(h * HEAD_DIM, (h + 1) * HEAD_DIM)
        q_h = q_ref[:, cols]
        g_h = g_ref[:, cols]
        scores = lax.dot_general(q_h, key_cat, nt, preferred_element_type=jnp.float32) * scaling
        scores = jnp.where(allowed, scores, -1e30)
        row_max = jnp.max(scores, axis=1, keepdims=True)
        total = jnp.sum(jnp.where(allowed, jnp.exp(scores - row_max), 0.0), axis=1, keepdims=True)
        log_total = row_max + jnp.log(total)
        prob = jnp.where(allowed, jnp.exp(scores - log_total), 0.0)
        prob_half = prob.astype(jnp.bfloat16)
        output = jnp.dot(prob_half, value_cat, preferred_element_type=jnp.float32)
        output = output.astype(jnp.bfloat16).astype(jnp.float32)
        row_dot = jnp.sum(g_h.astype(jnp.float32) * output, axis=1, keepdims=True)
        prob_grad = lax.dot_general(g_h, value_cat, nt, preferred_element_type=jnp.float32)
        score_grad = (prob * (prob_grad - row_dot) * scaling).astype(jnp.bfloat16)
        dq_h = jnp.dot(score_grad, key_cat, preferred_element_type=jnp.float32)
        dq_ref[:, cols] = dq_h.astype(jnp.bfloat16)
        dk_scr[...] += lax.dot_general(score_grad, q_h, tn, preferred_element_type=jnp.float32)
        dv_scr[...] += lax.dot_general(prob_half, g_h, tn, preferred_element_type=jnp.float32)

    for e in range(chosen):
        s = slot_ref[n * chosen + e]
        rows = slice(e * BLOCK, (e + 1) * BLOCK)
        acc_ref[s, :, :HEAD_DIM] += dk_scr[rows, :]
        acc_ref[s, :, HEAD_DIM:] += dv_scr[rows, :]


def attention_terms(slots, usable, earlier, query_states, out_grad, kv_stock, chosen):
    tok_rows, q_cols = query_states.shape
    slot_count = kv_stock.shape[0]
    group = q_cols // HEAD_DIM
    blocks_here = tok_rows // BLOCK
    kernel = functools.partial(attn_kernel, chosen=chosen, group=group, scaling=1.0 / math.sqrt(HEAD_DIM))
    grid_spec = pltpu.PrefetchScalarGridSpec(
        num_scalar_prefetch=3,
        grid=(blocks_here,),
        in_specs=[
            pl.BlockSpec((BLOCK, q_cols), lambda n, *_: (n, 0)),
            pl.BlockSpec((BLOCK, q_cols), lambda n, *_: (n, 0)),
            pl.BlockSpec((slot_count, BLOCK, 2 * HEAD_DIM), lambda n, *_: (0, 0, 0)),
        ],
        out_specs=[
            pl.BlockSpec((BLOCK, q_cols), lambda n, *_: (n, 0)),
            pl.BlockSpec((slot_count, BLOCK, 2 * HEAD_DIM), lambda n, *_: (0, 0, 0)),
        ],
        scratch_shapes=[
            pltpu.VMEM((chosen * BLOCK, 2 * HEAD_DIM), jnp.bfloat16),
            pltpu.VMEM((chosen * BLOCK, HEAD_DIM), jnp.float32),
            pltpu.VMEM((chosen * BLOCK, HEAD_DIM), jnp.float32),
        ],
    )
    return pl.pallas_call(
        kernel,
        grid_spec=grid_spec,
        out_shape=[
            jax.ShapeDtypeStruct((tok_rows, q_cols), jnp.bfloat16),
            jax.ShapeDtypeStruct((slot_count, BLOCK, 2 * HEAD_DIM), jnp.float32),
        ],
        compiler_params=pltpu.CompilerParams(dimension_semantics=("arbitrary",)),
    )(slots, usable, earlier, query_states, out_grad, kv_stock)


def body(query_states, key_states, value_states, out_grad, block_lists):
    ctx_count = lax.axis_size("ctx")
    head_count = lax.axis_size("head")
    myself = lax.axis_index("ctx")
    tok_rows = query_states.shape[0]
    kv_cols = key_states.shape[1]
    blocks_here = tok_rows // BLOCK
    chosen = block_lists.shape[1]
    lists_by_dev = block_lists.reshape(ctx_count, blocks_here * chosen)
    slot_ids = jnp.arange(blocks_here, dtype=jnp.int32)
    distances = jnp.arange(1, REACH + 1, dtype=jnp.int32)
    targets = myself + distances
    target_ok = targets < ctx_count
    target_rows = jnp.take(lists_by_dev, jnp.minimum(targets, ctx_count - 1), axis=0)
    mine = target_rows // blocks_here == myself
    requested = jnp.max(jnp.where(mine, target_rows % blocks_here, -1), axis=1)
    requested = jnp.where(target_ok, requested, -1)
    kv_local = jnp.concatenate([key_states, value_states], axis=1).reshape(blocks_here, BLOCK, 2 * kv_cols)
    outgoing = jnp.take(kv_local, jnp.clip(requested, 0, blocks_here - 1), axis=0)
    arrivals = [from_behind(outgoing[d - 1], "ctx", d) for d in range(1, REACH + 1)]
    kv_stock = jnp.concatenate([kv_local, jnp.stack(arrivals, axis=0)], axis=0)

    own_entries = lax.dynamic_slice_in_dim(block_lists, myself * blocks_here, blocks_here, 0)
    block_ids = myself * blocks_here + slot_ids
    order_ids = jnp.arange(chosen, dtype=jnp.int32)
    repeat = (own_entries[:, :, None] == own_entries[:, None, :]) & (
        order_ids[None, None, :] < order_ids[None, :, None]
    )
    usable = jnp.logical_not(jnp.any(repeat, axis=2))
    earlier = own_entries < block_ids[:, None]
    behind = myself - own_entries // blocks_here
    slots = jnp.where(behind == 0, own_entries % blocks_here, blocks_here - 1 + behind)
    slots = jnp.clip(slots, 0, blocks_here + REACH - 1)

    query_local, acc = attention_terms(
        slots.reshape(-1).astype(jnp.int32),
        usable.reshape(-1).astype(jnp.int32),
        earlier.reshape(-1).astype(jnp.int32),
        query_states,
        out_grad,
        kv_stock,
        chosen,
    )
    query_grad = lax.all_to_all(query_local, "head", split_axis=0, concat_axis=1, tiled=True)

    sendback = acc[blocks_here:].astype(jnp.bfloat16)
    returned = [from_behind(sendback[d - 1], "ctx", -d) for d in range(1, REACH + 1)]
    arrived = jnp.stack(returned, axis=0).astype(jnp.float32)
    credit = (requested[None, :] == slot_ids[:, None]).astype(jnp.float32)
    totals = acc[:blocks_here] + jnp.sum(credit[:, :, None, None] * arrived[None], axis=1)
    kv_grad = totals.reshape(tok_rows, 2 * kv_cols).astype(jnp.bfloat16)
    kv_all = lax.all_to_all(kv_grad, "head", split_axis=0, concat_axis=1, tiled=True)
    kv_all = kv_all.reshape(tok_rows // head_count, head_count, 2, kv_cols)
    key_grad = kv_all[:, :, 0, :].reshape(tok_rows // head_count, head_count * kv_cols)
    value_grad = kv_all[:, :, 1, :].reshape(tok_rows // head_count, head_count * kv_cols)
    return (query_grad, key_grad, value_grad)


def solution(mesh):
    in_specs = (P("ctx", "head"), P("ctx", "head"), P("ctx", "head"), P("ctx", "head"), P())
    out_specs = (P(("ctx", "head"), None), P(("ctx", "head"), None), P(("ctx", "head"), None))
    return jax.shard_map(body, mesh=mesh, in_specs=in_specs, out_specs=out_specs, check_vma=False)
```

time: 165 us -> 157 us (0.952)
  the two profiles are of different devices: /device:TPU:64 before, /device:TPU:368 now
where the time goes in v1:
time: 157 us; the launch traced here: 156 us
  starting transfers between devices  63.8 us (41%)
  waiting for transfers between devices  39.1 us (25%)
  Pallas kernels  26.8 us (17%)
  blocking collectives  12.7 us (8%)
  local copies, waits for them, and re-layouts  7.91 us (5%)
  other arithmetic  4.77 us (3%)
    ppermute x16, starting transfers between devices, from_behind(): return lax.ppermute(x, axis, pairs)  59.2 us
    ppermute x16, waiting for transfers between devices, from_behind(): return lax.ppermute(x, axis, pairs)  29.2 us
    pallas_call x1, Pallas kernels, attention_terms(): pl.pallas_call(kernel, grid_spec=grid_spec, out_shape=[jax.ShapeDtypeStru...  26.8 us
    all_to_all x1, blocking collectives, body(): lax.all_to_all(kv_grad, 'head', split_axis=0, concat_axis=1, tiled=True)  12.7 us
    all_to_all x1, waiting for transfers between devices, body(): lax.all_to_all(query_local, 'head', split_axis=0, concat_axis=1, tiled=True)  9.89 us
    all_to_all x1, starting transfers between devices, body(): lax.all_to_all(query_local, 'head', split_axis=0, concat_axis=1, tiled=True)  4.66 us
  transfers between devices with their start and end apart: 17, of which 8 were waited for; matrix products, arithmetic and copies ran while one was open for 3% of the time, Pallas kernels for 0%

profile of v1, /device:TPU:368, one launch (start us, length us, event | category | flops | bytes accessed | tf_op | source)
XLA Modules:
  0.0 156.1 jit_solution(1108313546407810273)
XLA Ops:
  0.7 0.8 copy.28
  1.6 0.6 gather_fusion
  2.2 0.2 fusion.2
  2.4 1.0 pad_maximum_fusion
  3.4 0.6 gather_fusion.1
  4.0 0.1 broadcast_select_fusion
  4.2 3.4 %collective-permute-start.7 = (bf16[128,256]{1,0:T(8,128)(2,1)S(1)}, bf16[128,256]{1,0:T(8,128)(2,1)S(1)}, u32[]{:S(2)}, u32[]{:S(2)}) collective-permute-start(bf16[128,256]{1,0:T(8,128)(2,1)S(1)} %get-tuple-element.19), channel_id=1, source_target_pairs={{0,64},{8,72},{16,80},{24,88},{32,96},{40,104},{48,112},{56,120},{... | collective-permute-start | bytes 196616 | tf_op jit(solution)/shard_map/ppermute | solution.py:21
  7.6 2.3 %collective-permute-start.6 = (bf16[128,256]{1,0:T(8,128)(2,1)S(1)}, bf16[128,256]{1,0:T(8,128)(2,1)S(1)}, u32[]{:S(2)}, u32[]{:S(2)}) collective-permute-start(bf16[128,256]{1,0:T(8,128)(2,1)S(1)} %get-tuple-element.20), channel_id=1, source_target_pairs={{0,56},{8,64},{16,72},{24,80},{32,88},{40,96},{48,104},{56,112},{6... | collective-permute-start | bytes 196616 | tf_op jit(solution)/shard_map/ppermute | solution.py:21
  9.9 3.7 %collective-permute-start.5 = (bf16[128,256]{1,0:T(8,128)(2,1)S(1)}, bf16[128,256]{1,0:T(8,128)(2,1)S(1)}, u32[]{:S(2)}, u32[]{:S(2)}) collective-permute-start(bf16[128,256]{1,0:T(8,128)(2,1)S(1)} %get-tuple-element.21), channel_id=1, source_target_pairs={{0,48},{8,56},{16,64},{24,72},{32,80},{40,88},{48,96},{56,104},{64... | collective-permute-start | bytes 196616 | tf_op jit(solution)/shard_map/ppermute | solution.py:21
  13.6 1.9 %collective-permute-start.4 = (bf16[128,256]{1,0:T(8,128)(2,1)S(1)}, bf16[128,256]{1,0:T(8,128)(2,1)S(1)}, u32[]{:S(2)}, u32[]{:S(2)}) collective-permute-start(bf16[128,256]{1,0:T(8,128)(2,1)S(1)} %get-tuple-element.22), channel_id=1, source_target_pairs={{0,40},{8,48},{16,56},{24,64},{32,72},{40,80},{48,88},{56,96},{64,... | collective-permute-start | bytes 196616 | tf_op jit(solution)/shard_map/ppermute | solution.py:21
  15.6 2.0 %collective-permute-start = (bf16[128,256]{1,0:T(8,128)(2,1)S(1)}, bf16[128,256]{1,0:T(8,128)(2,1)S(1)}, u32[]{:S(2)}, u32[]{:S(2)}) collective-permute-start(bf16[128,256]{1,0:T(8,128)(2,1)S(1)} %get-tuple-element.26), channel_id=1, source_target_pairs={{0,8},{8,16},{16,24},{24,32},{32,40},{40,48},{48,56},{56,64},{64,7... | collective-permute-start | bytes 196616 | tf_op jit(solution)/shard_map/ppermute | solution.py:21
  17.7 0.1 copy.25
  17.8 0.1 copy.27
  17.9 0.7 reshape.212.early_ref
  18.7 0.6 reshape.207.slot_ref
  19.3 0.2 and_reduce_fusion
  19.5 0.6 reshape.211.use_ref
  20.1 3.0 %collective-permute-done = bf16[128,256]{1,0:T(8,128)(2,1)S(1)} collective-permute-done((bf16[128,256]{1,0:T(8,128)(2,1)S(1)}, bf16[128,256]{1,0:T(8,128)(2,1)S(1)}, u32[]{:S(2)}, u32[]{:S(2)}) %collective-permute-start) | collective-permute-done | bytes 65568 | tf_op jit(solution)/shard_map/ppermute | solution.py:21
  23.1 6.1 %collective-permute-start.1 = (bf16[128,256]{1,0:T(8,128)(2,1)S(1)}, bf16[128,256]{1,0:T(8,128)(2,1)S(1)}, u32[]{:S(2)}, u32[]{:S(2)}) collective-permute-start(bf16[128,256]{1,0:T(8,128)(2,1)S(1)} %get-tuple-element.25), channel_id=1, source_target_pairs={{0,16},{8,24},{16,32},{24,40},{32,48},{40,56},{48,64},{56,72},{64,... | collective-permute-start | bytes 196616 | tf_op jit(solution)/shard_map/ppermute | solution.py:21
  29.2 1.9 %collective-permute-done.1 = bf16[128,256]{1,0:T(8,128)(2,1)S(1)} collective-permute-done((bf16[128,256]{1,0:T(8,128)(2,1)S(1)}, bf16[128,256]{1,0:T(8,128)(2,1)S(1)}, u32[]{:S(2)}, u32[]{:S(2)}) %collective-permute-start.1) | collective-permute-done | bytes 65568 | tf_op jit(solution)/shard_map/ppermute | solution.py:21
  31.1 3.1 %collective-permute-start.2 = (bf16[128,256]{1,0:T(8,128)(2,1)S(1)}, bf16[128,256]{1,0:T(8,128)(2,1)S(1)}, u32[]{:S(2)}, u32[]{:S(2)}) collective-permute-start(bf16[128,256]{1,0:T(8,128)(2,1)S(1)} %get-tuple-element.24), channel_id=1, source_target_pairs={{0,24},{8,32},{16,40},{24,48},{32,56},{40,64},{48,72},{56,80},{64,... | collective-permute-start | bytes 196616 | tf_op jit(solution)/shard_map/ppermute | solution.py:21
  34.3 2.5 %collective-permute-done.2 = bf16[128,256]{1,0:T(8,128)(2,1)S(1)} collective-permute-done((bf16[128,256]{1,0:T(8,128)(2,1)S(1)}, bf16[128,256]{1,0:T(8,128)(2,1)S(1)}, u32[]{:S(2)}, u32[]{:S(2)}) %collective-permute-start.2) | collective-permute-done | bytes 65568 | tf_op jit(solution)/shard_map/ppermute | solution.py:21
  36.8 3.9 %collective-permute-start.3 = (bf16[128,256]{1,0:T(8,128)(2,1)S(1)}, bf16[128,256]{1,0:T(8,128)(2,1)S(1)}, u32[]{:S(2)}, u32[]{:S(2)}) collective-permute-start(bf16[128,256]{1,0:T(8,128)(2,1)S(1)} %get-tuple-element.23), channel_id=1, source_target_pairs={{0,32},{8,40},{16,48},{24,56},{32,64},{40,72},{48,80},{56,88},{64,... | collective-permute-start | bytes 196616 | tf_op jit(solution)/shard_map/ppermute | solution.py:21
  40.7 2.8 %collective-permute-done.3 = bf16[128,256]{1,0:T(8,128)(2,1)S(1)} collective-permute-done((bf16[128,256]{1,0:T(8,128)(2,1)S(1)}, bf16[128,256]{1,0:T(8,128)(2,1)S(1)}, u32[]{:S(2)}, u32[]{:S(2)}) %collective-permute-start.3) | collective-permute-done | bytes 65568 | tf_op jit(solution)/shard_map/ppermute | solution.py:21
  43.7 0.9 copy-done
  44.6 26.8 %shard_map.76 = (bf16[512,1024]{1,0:T(8,128)(2,1)}, f32[12,128,256]{2,1,0:T(8,128)}) custom-call(s32[16]{0:T(128)} %reshape.207.slot_ref, s32[16]{0:T(128)} %reshape.211.use_ref, s32[16]{0:T(128)} %reshape.212.early_ref, bf16[512,1024]{1,0:T(8,128)(2,1)} %q_ref.1, bf16[512,1024]{1,0:T(8,128)(2,1)} %g_ref.1, bf16[12,128,256]{2,1,0:T(8,128)(2,1)} %copy-done), custom_call_target="tpu_custom_call" | custom-call | tf_op jit(solution)/shard_map/pallas_call | solution.py:105
  71.3 1.5 convert.5
  72.9 4.7 %collective-permute-start.8 = (bf16[128,256]{1,0:T(8,128)(2,1)S(1)}, bf16[128,256]{1,0:T(8,128)(2,1)S(1)}, u32[]{:S(2)}, u32[]{:S(2)}) collective-permute-start(bf16[128,256]{1,0:T(8,128)(2,1)S(1)} %get-tuple-element.18), channel_id=1, source_target_pairs={{8,0},{16,8},{24,16},{32,24},{40,32},{48,40},{56,48},{64,56},{72,6... | collective-permute-start | bytes 196616 | tf_op jit(solution)/shard_map/ppermute | solution.py:21
  77.6 4.6 %collective-permute-start.15 = (bf16[128,256]{1,0:T(8,128)(2,1)S(1)}, bf16[128,256]{1,0:T(8,128)(2,1)S(1)}, u32[]{:S(2)}, u32[]{:S(2)}) collective-permute-start(bf16[128,256]{1,0:T(8,128)(2,1)S(1)} %get-tuple-element.11), channel_id=1, source_target_pairs={{64,0},{72,8},{80,16},{88,24},{96,32},{104,40},{112,48},{120,56},{... | collective-permute-start | bytes 196616 | tf_op jit(solution)/shard_map/ppermute | solution.py:21
  82.2 2.4 %collective-permute-start.14 = (bf16[128,256]{1,0:T(8,128)(2,1)S(1)}, bf16[128,256]{1,0:T(8,128)(2,1)S(1)}, u32[]{:S(2)}, u32[]{:S(2)}) collective-permute-start(bf16[128,256]{1,0:T(8,128)(2,1)S(1)} %get-tuple-element.12), channel_id=1, source_target_pairs={{56,0},{64,8},{72,16},{80,24},{88,32},{96,40},{104,48},{112,56},{1... | collective-permute-start | bytes 196616 | tf_op jit(solution)/shard_map/ppermute | solution.py:21
  84.6 6.7 %collective-permute-start.13 = (bf16[128,256]{1,0:T(8,128)(2,1)S(1)}, bf16[128,256]{1,0:T(8,128)(2,1)S(1)}, u32[]{:S(2)}, u32[]{:S(2)}) collective-permute-start(bf16[128,256]{1,0:T(8,128)(2,1)S(1)} %get-tuple-element.13), channel_id=1, source_target_pairs={{48,0},{56,8},{64,16},{72,24},{80,32},{88,40},{96,48},{104,56},{11... | collective-permute-start | bytes 196616 | tf_op jit(solution)/shard_map/ppermute | solution.py:21
  91.3 6.9 %collective-permute-start.12 = (bf16[128,256]{1,0:T(8,128)(2,1)S(1)}, bf16[128,256]{1,0:T(8,128)(2,1)S(1)}, u32[]{:S(2)}, u32[]{:S(2)}) collective-permute-start(bf16[128,256]{1,0:T(8,128)(2,1)S(1)} %get-tuple-element.14), channel_id=1, source_target_pairs={{40,0},{48,8},{56,16},{64,24},{72,32},{80,40},{88,48},{96,56},{104... | collective-permute-start | bytes 196616 | tf_op jit(solution)/shard_map/ppermute | solution.py:21
  98.2 3.5 %collective-permute-start.9 = (bf16[128,256]{1,0:T(8,128)(2,1)S(1)}, bf16[128,256]{1,0:T(8,128)(2,1)S(1)}, u32[]{:S(2)}, u32[]{:S(2)}) collective-permute-start(bf16[128,256]{1,0:T(8,128)(2,1)S(1)} %get-tuple-element.17), channel_id=1, source_target_pairs={{16,0},{24,8},{32,16},{40,24},{48,32},{56,40},{64,48},{72,56},{80,... | collective-permute-start | bytes 196616 | tf_op jit(solution)/shard_map/ppermute | solution.py:21
  101.8 6.3 %collective-permute-done.9 = bf16[128,256]{1,0:T(8,128)(2,1)S(1)} collective-permute-done((bf16[128,256]{1,0:T(8,128)(2,1)S(1)}, bf16[128,256]{1,0:T(8,128)(2,1)S(1)}, u32[]{:S(2)}, u32[]{:S(2)}) %collective-permute-start.9) | collective-permute-done | bytes 65568 | tf_op jit(solution)/shard_map/ppermute | solution.py:21
  108.0 1.9 %collective-permute-start.10 = (bf16[128,256]{1,0:T(8,128)(2,1)S(1)}, bf16[128,256]{1,0:T(8,128)(2,1)S(1)}, u32[]{:S(2)}, u32[]{:S(2)}) collective-permute-start(bf16[128,256]{1,0:T(8,128)(2,1)S(1)} %get-tuple-element.16), channel_id=1, source_target_pairs={{24,0},{32,8},{40,16},{48,24},{56,32},{64,40},{72,48},{80,56},{88,... | collective-permute-start | bytes 196616 | tf_op jit(solution)/shard_map/ppermute | solution.py:21
  109.9 7.3 %collective-permute-done.10 = bf16[128,256]{1,0:T(8,128)(2,1)S(1)} collective-permute-done((bf16[128,256]{1,0:T(8,128)(2,1)S(1)}, bf16[128,256]{1,0:T(8,128)(2,1)S(1)}, u32[]{:S(2)}, u32[]{:S(2)}) %collective-permute-start.10) | collective-permute-done | bytes 65568 | tf_op jit(solution)/shard_map/ppermute | solution.py:21
  117.2 1.9 %collective-permute-start.11 = (bf16[128,256]{1,0:T(8,128)(2,1)S(1)}, bf16[128,256]{1,0:T(8,128)(2,1)S(1)}, u32[]{:S(2)}, u32[]{:S(2)}) collective-permute-start(bf16[128,256]{1,0:T(8,128)(2,1)S(1)} %get-tuple-element.15), channel_id=1, source_target_pairs={{32,0},{40,8},{48,16},{56,24},{64,32},{72,40},{80,48},{88,56},{96,... | collective-permute-start | bytes 196616 | tf_op jit(solution)/shard_map/ppermute | solution.py:21
  119.1 5.4 %collective-permute-done.11 = bf16[128,256]{1,0:T(8,128)(2,1)S(1)} collective-permute-done((bf16[128,256]{1,0:T(8,128)(2,1)S(1)}, bf16[128,256]{1,0:T(8,128)(2,1)S(1)}, u32[]{:S(2)}, u32[]{:S(2)}) %collective-permute-start.11) | collective-permute-done | bytes 65568 | tf_op jit(solution)/shard_map/ppermute | solution.py:21
  124.8 0.4 multiply_reduce_fusion
  125.1 1.1 add_convert_fusion
  126.2 12.7 %all_to_all.32 = bf16[8,64,256]{2,1,0:T(8,128)(2,1)S(1)} all-to-all(bf16[8,64,256]{2,1,0:T(8,128)(2,1)S(1)} %bitcast.94), channel_id=1, replica_groups=mesh['ctx'=64,'head'=8] {'head'}, dimensions={0} | all-to-all | bytes 524288 | tf_op jit(solution)/shard_map/all_to_all | solution.py:167
  138.9 4.7 %all-to-all-start = ((bf16[8,64,1024]{2,1,0:T(8,128)(2,1)}), bf16[8,64,1024]{2,1,0:T(8,128)(2,1)S(1)}, u32[]{:S(2)}, u32[]{:S(2)}) async-start(bf16[8,64,1024]{2,1,0:T(8,128)(2,1)} %bitcast.20), calls=%async_computation | async-start | bytes 2097152 | tf_op jit(solution)/shard_map/all_to_all | solution.py:159
  143.6 0.5 fusion.13
  144.1 0.2 copy.33
  144.3 0.2 copy.32
  144.4 0.7 copy_bitcast_fusion
  145.2 9.9 %all-to-all-done = bf16[8,64,1024]{2,1,0:T(8,128)(2,1)S(1)} async-done(((bf16[8,64,1024]{2,1,0:T(8,128)(2,1)}), bf16[8,64,1024]{2,1,0:T(8,128)(2,1)S(1)}, u32[]{:S(2)}, u32[]{:S(2)}) %all-to-all-start) | async-done | bytes 1048608 | tf_op jit(solution)/shard_map/all_to_all | solution.py:159
  155.1 1.1 copy.34
  (47 shorter events, 0.7 us)
Async XLA Ops:
  3.4 14.2 %copy-start.1 = (s32[256,4]{0,1:T(4,128)S(1)}, s32[256,4]{0,1:T(4,128)}, u32[]{:S(2)}) copy-start(s32[256,4]{0,1:T(4,128)} %param.9) | copy-start | bytes 12292
  4.2 39.5 %collective-permute-start.7 = (bf16[128,256]{1,0:T(8,128)(2,1)S(1)}, bf16[128,256]{1,0:T(8,128)(2,1)S(1)}, u32[]{:S(2)}, u32[]{:S(2)}) collective-permute-start(bf16[128,256]{1,0:T(8,128)(2,1)S(1)} %get-tuple-element.19), channel_id=1, source_target_pairs={{0,64},{8,72},{16,80},{24,88},{32,96},{40,104},{48,112},{56,120},{... | collective-permute-start | bytes 196616 | tf_op jit(solution)/shard_map/ppermute | solution.py:21
  7.6 36.1 %collective-permute-start.6 = (bf16[128,256]{1,0:T(8,128)(2,1)S(1)}, bf16[128,256]{1,0:T(8,128)(2,1)S(1)}, u32[]{:S(2)}, u32[]{:S(2)}) collective-permute-start(bf16[128,256]{1,0:T(8,128)(2,1)S(1)} %get-tuple-element.20), channel_id=1, source_target_pairs={{0,56},{8,64},{16,72},{24,80},{32,88},{40,96},{48,104},{56,112},{6... | collective-permute-start | bytes 196616 | tf_op jit(solution)/shard_map/ppermute | solution.py:21
  9.9 33.7 %collective-permute-start.5 = (bf16[128,256]{1,0:T(8,128)(2,1)S(1)}, bf16[128,256]{1,0:T(8,128)(2,1)S(1)}, u32[]{:S(2)}, u32[]{:S(2)}) collective-permute-start(bf16[128,256]{1,0:T(8,128)(2,1)S(1)} %get-tuple-element.21), channel_id=1, source_target_pairs={{0,48},{8,56},{16,64},{24,72},{32,80},{40,88},{48,96},{56,104},{64... | collective-permute-start | bytes 196616 | tf_op jit(solution)/shard_map/ppermute | solution.py:21
  13.6 29.9 %collective-permute-start.4 = (bf16[128,256]{1,0:T(8,128)(2,1)S(1)}, bf16[128,256]{1,0:T(8,128)(2,1)S(1)}, u32[]{:S(2)}, u32[]{:S(2)}) collective-permute-start(bf16[128,256]{1,0:T(8,128)(2,1)S(1)} %get-tuple-element.22), channel_id=1, source_target_pairs={{0,40},{8,48},{16,56},{24,64},{32,72},{40,80},{48,88},{56,96},{64,... | collective-permute-start | bytes 196616 | tf_op jit(solution)/shard_map/ppermute | solution.py:21
  15.6 7.5 %collective-permute-start = (bf16[128,256]{1,0:T(8,128)(2,1)S(1)}, bf16[128,256]{1,0:T(8,128)(2,1)S(1)}, u32[]{:S(2)}, u32[]{:S(2)}) collective-permute-start(bf16[128,256]{1,0:T(8,128)(2,1)S(1)} %get-tuple-element.26), channel_id=1, source_target_pairs={{0,8},{8,16},{16,24},{24,32},{32,40},{40,48},{48,56},{56,64},{64,7... | collective-permute-start | bytes 196616 | tf_op jit(solution)/shard_map/ppermute | solution.py:21
  23.1 8.0 %collective-permute-start.1 = (bf16[128,256]{1,0:T(8,128)(2,1)S(1)}, bf16[128,256]{1,0:T(8,128)(2,1)S(1)}, u32[]{:S(2)}, u32[]{:S(2)}) collective-permute-start(bf16[128,256]{1,0:T(8,128)(2,1)S(1)} %get-tuple-element.25), channel_id=1, source_target_pairs={{0,16},{8,24},{16,32},{24,40},{32,48},{40,56},{48,64},{56,72},{64,... | collective-permute-start | bytes 196616 | tf_op jit(solution)/shard_map/ppermute | solution.py:21
  31.1 5.7 %collective-permute-start.2 = (bf16[128,256]{1,0:T(8,128)(2,1)S(1)}, bf16[128,256]{1,0:T(8,128)(2,1)S(1)}, u32[]{:S(2)}, u32[]{:S(2)}) collective-permute-start(bf16[128,256]{1,0:T(8,128)(2,1)S(1)} %get-tuple-element.24), channel_id=1, source_target_pairs={{0,24},{8,32},{16,40},{24,48},{32,56},{40,64},{48,72},{56,80},{64,... | collective-permute-start | bytes 196616 | tf_op jit(solution)/shard_map/ppermute | solution.py:21
  36.8 6.8 %collective-permute-start.3 = (bf16[128,256]{1,0:T(8,128)(2,1)S(1)}, bf16[128,256]{1,0:T(8,128)(2,1)S(1)}, u32[]{:S(2)}, u32[]{:S(2)}) collective-permute-start(bf16[128,256]{1,0:T(8,128)(2,1)S(1)} %get-tuple-element.23), channel_id=1, source_target_pairs={{0,32},{8,40},{16,48},{24,56},{32,64},{40,72},{48,80},{56,88},{64,... | collective-permute-start | bytes 196616 | tf_op jit(solution)/shard_map/ppermute | solution.py:21
  43.7 0.9 copy-start
  72.9 25.4 %collective-permute-start.8 = (bf16[128,256]{1,0:T(8,128)(2,1)S(1)}, bf16[128,256]{1,0:T(8,128)(2,1)S(1)}, u32[]{:S(2)}, u32[]{:S(2)}) collective-permute-start(bf16[128,256]{1,0:T(8,128)(2,1)S(1)} %get-tuple-element.18), channel_id=1, source_target_pairs={{8,0},{16,8},{24,16},{32,24},{40,32},{48,40},{56,48},{64,56},{72,6... | collective-permute-start | bytes 196616 | tf_op jit(solution)/shard_map/ppermute | solution.py:21
  77.6 47.1 %collective-permute-start.15 = (bf16[128,256]{1,0:T(8,128)(2,1)S(1)}, bf16[128,256]{1,0:T(8,128)(2,1)S(1)}, u32[]{:S(2)}, u32[]{:S(2)}) collective-permute-start(bf16[128,256]{1,0:T(8,128)(2,1)S(1)} %get-tuple-element.11), channel_id=1, source_target_pairs={{64,0},{72,8},{80,16},{88,24},{96,32},{104,40},{112,48},{120,56},{... | collective-permute-start | bytes 196616 | tf_op jit(solution)/shard_map/ppermute | solution.py:21
  82.2 42.4 %collective-permute-start.14 = (bf16[128,256]{1,0:T(8,128)(2,1)S(1)}, bf16[128,256]{1,0:T(8,128)(2,1)S(1)}, u32[]{:S(2)}, u32[]{:S(2)}) collective-permute-start(bf16[128,256]{1,0:T(8,128)(2,1)S(1)} %get-tuple-element.12), channel_id=1, source_target_pairs={{56,0},{64,8},{72,16},{80,24},{88,32},{96,40},{104,48},{112,56},{1... | collective-permute-start | bytes 196616 | tf_op jit(solution)/shard_map/ppermute | solution.py:21
  84.6 40.0 %collective-permute-start.13 = (bf16[128,256]{1,0:T(8,128)(2,1)S(1)}, bf16[128,256]{1,0:T(8,128)(2,1)S(1)}, u32[]{:S(2)}, u32[]{:S(2)}) collective-permute-start(bf16[128,256]{1,0:T(8,128)(2,1)S(1)} %get-tuple-element.13), channel_id=1, source_target_pairs={{48,0},{56,8},{64,16},{72,24},{80,32},{88,40},{96,48},{104,56},{11... | collective-permute-start | bytes 196616 | tf_op jit(solution)/shard_map/ppermute | solution.py:21
  91.3 33.2 %collective-permute-start.12 = (bf16[128,256]{1,0:T(8,128)(2,1)S(1)}, bf16[128,256]{1,0:T(8,128)(2,1)S(1)}, u32[]{:S(2)}, u32[]{:S(2)}) collective-permute-start(bf16[128,256]{1,0:T(8,128)(2,1)S(1)} %get-tuple-element.14), channel_id=1, source_target_pairs={{40,0},{48,8},{56,16},{64,24},{72,32},{80,40},{88,48},{96,56},{104... | collective-permute-start | bytes 196616 | tf_op jit(solution)/shard_map/ppermute | solution.py:21
  98.2 9.8 %collective-permute-start.9 = (bf16[128,256]{1,0:T(8,128)(2,1)S(1)}, bf16[128,256]{1,0:T(8,128)(2,1)S(1)}, u32[]{:S(2)}, u32[]{:S(2)}) collective-permute-start(bf16[128,256]{1,0:T(8,128)(2,1)S(1)} %get-tuple-element.17), channel_id=1, source_target_pairs={{16,0},{24,8},{32,16},{40,24},{48,32},{56,40},{64,48},{72,56},{80,... | collective-permute-start | bytes 196616 | tf_op jit(solution)/shard_map/ppermute | solution.py:21
  108.0 9.2 %collective-permute-start.10 = (bf16[128,256]{1,0:T(8,128)(2,1)S(1)}, bf16[128,256]{1,0:T(8,128)(2,1)S(1)}, u32[]{:S(2)}, u32[]{:S(2)}) collective-permute-start(bf16[128,256]{1,0:T(8,128)(2,1)S(1)} %get-tuple-element.16), channel_id=1, source_target_pairs={{24,0},{32,8},{40,16},{48,24},{56,32},{64,40},{72,48},{80,56},{88,... | collective-permute-start | bytes 196616 | tf_op jit(solution)/shard_map/ppermute | solution.py:21
  117.2 7.4 %collective-permute-start.11 = (bf16[128,256]{1,0:T(8,128)(2,1)S(1)}, bf16[128,256]{1,0:T(8,128)(2,1)S(1)}, u32[]{:S(2)}, u32[]{:S(2)}) collective-permute-start(bf16[128,256]{1,0:T(8,128)(2,1)S(1)} %get-tuple-element.15), channel_id=1, source_target_pairs={{32,0},{40,8},{48,16},{56,24},{64,32},{72,40},{80,48},{88,56},{96,... | collective-permute-start | bytes 196616 | tf_op jit(solution)/shard_map/ppermute | solution.py:21
  138.9 16.2 %all-to-all-start = ((bf16[8,64,1024]{2,1,0:T(8,128)(2,1)}), bf16[8,64,1024]{2,1,0:T(8,128)(2,1)S(1)}, u32[]{:S(2)}, u32[]{:S(2)}) async-start(bf16[8,64,1024]{2,1,0:T(8,128)(2,1)} %bitcast.20), calls=%async_computation | async-start | bytes 2097152 | tf_op jit(solution)/shard_map/all_to_all | solution.py:159

commit v2 on v1

--- a/solution.py
+++ b/solution.py
@@ -19,6 +19,22 @@
     devices = lax.axis_size(axis)
     pairs = [(i, i + by) for i in range(devices) if 0 <= i + by < devices]
     return lax.ppermute(x, axis, pairs)
+
+
+def fetch_tree(outgoing):
+    step1 = from_behind(outgoing[jnp.array([0, 2, 4, 6])], "ctx", 1)
+    step2 = from_behind(jnp.stack([outgoing[1], step1[1], outgoing[5], step1[3]]), "ctx", 2)
+    step4 = from_behind(jnp.stack([outgoing[3], step1[2], step2[2], step2[3]]), "ctx", 4)
+    step8 = from_behind(outgoing[7], "ctx", 8)
+    return jnp.stack([step1[0], step2[0], step2[1], step4[0], step4[1], step4[2], step4[3], step8])
+
+
+def return_tree(sendback):
+    step4 = from_behind(sendback[3:7], "ctx", -4)
+    step2 = from_behind(jnp.stack([sendback[1], sendback[2], step4[2], step4[3]]), "ctx", -2)
+    step1 = from_behind(jnp.stack([sendback[0], step2[1], step4[1], step2[3]]), "ctx", -1)
+    step8 = from_behind(sendback[7], "ctx", -8)
+    return jnp.stack([step1[0], step2[0], step1[1], step4[0], step1[2], step2[2], step1[3], step8])
 
 
 def attn_kernel(slot_ref, use_ref, early_ref, q_ref, g_ref, kv_ref, dq_ref, acc_ref, kv_scr, dk_scr, dv_scr,
@@ -57,9 +73,9 @@
         scores = lax.dot_general(q_h, key_cat, nt, preferred_element_type=jnp.float32) * scaling
         scores = jnp.where(allowed, scores, -1e30)
         row_max = jnp.max(scores, axis=1, keepdims=True)
-        total = jnp.sum(jnp.where(allowed, jnp.exp(scores - row_max), 0.0), axis=1, keepdims=True)
+        total = jnp.sum(jnp.exp(scores - row_max), axis=1, keepdims=True)
         log_total = row_max + jnp.log(total)
-        prob = jnp.where(allowed, jnp.exp(scores - log_total), 0.0)
+        prob = jnp.exp(scores - log_total)
         prob_half = prob.astype(jnp.bfloat16)
         output = jnp.dot(prob_half, value_cat, preferred_element_type=jnp.float32)
         output = output.astype(jnp.bfloat16).astype(jnp.float32)
@@ -132,8 +148,7 @@
     requested = jnp.where(target_ok, requested, -1)
     kv_local = jnp.concatenate([key_states, value_states], axis=1).reshape(blocks_here, BLOCK, 2 * kv_cols)
     outgoing = jnp.take(kv_local, jnp.clip(requested, 0, blocks_here - 1), axis=0)
-    arrivals = [from_behind(outgoing[d - 1], "ctx", d) for d in range(1, REACH + 1)]
-    kv_stock = jnp.concatenate([kv_local, jnp.stack(arrivals, axis=0)], axis=0)
+    kv_stock = jnp.concatenate([kv_local, fetch_tree(outgoing)], axis=0)
 
     own_entries = lax.dynamic_slice_in_dim(block_lists, myself * blocks_here, blocks_here, 0)
     block_ids = myself * blocks_here + slot_ids
@@ -156,18 +171,19 @@
         kv_stock,
         chosen,
     )
-    query_grad = lax.all_to_all(query_local, "head", split_axis=0, concat_axis=1, tiled=True)
-
     sendback = acc[blocks_here:].astype(jnp.bfloat16)
-    returned = [from_behind(sendback[d - 1], "ctx", -d) for d in range(1, REACH + 1)]
-    arrived = jnp.stack(returned, axis=0).astype(jnp.float32)
+    arrived = return_tree(sendback).astype(jnp.float32)
     credit = (requested[None, :] == slot_ids[:, None]).astype(jnp.float32)
     totals = acc[:blocks_here] + jnp.sum(credit[:, :, None, None] * arrived[None], axis=1)
     kv_grad = totals.reshape(tok_rows, 2 * kv_cols).astype(jnp.bfloat16)
-    kv_all = lax.all_to_all(kv_grad, "head", split_axis=0, concat_axis=1, tiled=True)
-    kv_all = kv_all.reshape(tok_rows // head_count, head_count, 2, kv_cols)
-    key_grad = kv_all[:, :, 0, :].reshape(tok_rows // head_count, head_count * kv_cols)
-    value_grad = kv_all[:, :, 1, :].reshape(tok_rows // head_count, head_count * kv_cols)
+    q_cols = query_local.shape[1]
+    both = jnp.concatenate([query_local, kv_grad], axis=1)
+    both = lax.all_to_all(both, "head", split_axis=0, concat_axis=1, tiled=True)
+    both = both.reshape(tok_rows // head_count, head_count, q_cols + 2 * kv_cols)
+    out_rows = tok_rows // head_count
+    query_grad = both[:, :, :q_cols].reshape(out_rows, head_count * q_cols)
+    key_grad = both[:, :, q_cols:q_cols + kv_cols].reshape(out_rows, head_count * kv_cols)
+    value_grad = both[:, :, q_cols + kv_cols:].reshape(out_rows, head_count * kv_cols)
     return (query_grad, key_grad, value_grad)
 
 

time: 157 us -> 129 us (0.82)
  the two profiles are of different devices: /device:TPU:368 before, /device:TPU:192 now
where the time goes in v2:
time: 129 us; the launch traced here: 128 us
  waiting for transfers between devices  39.4 us (31%)
  Pallas kernels  26.3 us (20%)
  starting transfers between devices  24.8 us (19%)
  blocking collectives  23.1 us (18%)
  local copies, waits for them, and re-layouts  8.4 us (7%)
  other arithmetic  4.99 us (4%)
    ppermute x8, waiting for transfers between devices, from_behind(): return lax.ppermute(x, axis, pairs)  39.4 us
    pallas_call x1, Pallas kernels, attention_terms(): pl.pallas_call(kernel, grid_spec=grid_spec, out_shape=[jax.ShapeDtypeStru...  26.3 us
    ppermute x8, starting transfers between devices, from_behind(): return lax.ppermute(x, axis, pairs)  24.8 us
    all_to_all x1, blocking collectives, body(): both = lax.all_to_all(both, 'head', split_axis=0, concat_axis=1, tiled=True)  23.1 us
  transfers between devices with their start and end apart: 8, of which 7 were waited for; matrix products, arithmetic and copies ran while one was open for 2% of the time, Pallas kernels for 0%

profile of v2, /device:TPU:192, one launch (start us, length us, event | category | flops | bytes accessed | tf_op | source)
XLA Modules:
  0.0 128.1 jit_solution(17585536319795794866)
XLA Ops:
  0.7 0.8 copy.29
  1.5 0.1 reshape.205
  1.6 0.6 gather_fusion
  2.2 0.2 fusion.2
  2.4 1.0 pad_maximum_fusion.1
  3.4 0.6 gather_fusion.1
  4.0 0.0 copy-start.2
  4.0 0.1 broadcast_select_fusion
  4.1 0.6 gather_fusion.2
  4.7 1.9 %collective-permute-start = (bf16[4,128,256]{2,1,0:T(8,128)(2,1)S(1)}, bf16[4,128,256]{2,1,0:T(8,128)(2,1)S(1)}, u32[]{:S(2)}, u32[]{:S(2)}) collective-permute-start(bf16[4,128,256]{2,1,0:T(8,128)(2,1)S(1)} %gather_fusion.2), channel_id=1, source_target_pairs={{0,8},{8,16},{16,24},{24,32},{32,40},{40,48},{48,56},{56,64},{64,7... | collective-permute-start | bytes 786440 | tf_op jit(solution)/shard_map/ppermute | solution.py:21
  6.7 6.4 %collective-permute-start.3 = (bf16[128,256]{1,0:T(8,128)(2,1)S(1)}, bf16[128,256]{1,0:T(8,128)(2,1)S(1)}, u32[]{:S(2)}, u32[]{:S(2)}) collective-permute-start(bf16[128,256]{1,0:T(8,128)(2,1)S(1)} %get-tuple-element.15), channel_id=1, source_target_pairs={{0,64},{8,72},{16,80},{24,88},{32,96},{40,104},{48,112},{56,120},{... | collective-permute-start | bytes 196616 | tf_op jit(solution)/shard_map/ppermute | solution.py:21
  13.1 0.1 compare_convert_fusion
  13.2 1.6 %collective-permute-done = bf16[4,128,256]{2,1,0:T(8,128)(2,1)S(1)} collective-permute-done((bf16[4,128,256]{2,1,0:T(8,128)(2,1)S(1)}, bf16[4,128,256]{2,1,0:T(8,128)(2,1)S(1)}, u32[]{:S(2)}, u32[]{:S(2)}) %collective-permute-start) | collective-permute-done | bytes 262176 | tf_op jit(solution)/shard_map/ppermute | solution.py:21
  14.9 4.2 %collective-permute-start.1 = (bf16[4,128,256]{2,1,0:T(8,128)(2,1)S(1)}, bf16[4,128,256]{2,1,0:T(8,128)(2,1)S(1)}, u32[]{:S(2)}, u32[]{:S(2)}) collective-permute-start(bf16[4,128,256]{2,1,0:T(8,128)(2,1)S(1)} %pad_maximum_fusion.2), channel_id=1, source_target_pairs={{0,16},{8,24},{16,32},{24,40},{32,48},{40,56},{48,64},{56,72},{64,... | collective-permute-start | bytes 786440 | tf_op jit(solution)/shard_map/ppermute | solution.py:21
  19.1 0.1 copy.26
  19.2 8.7 %collective-permute-done.1 = bf16[4,128,256]{2,1,0:T(8,128)(2,1)S(1)} collective-permute-done((bf16[4,128,256]{2,1,0:T(8,128)(2,1)S(1)}, bf16[4,128,256]{2,1,0:T(8,128)(2,1)S(1)}, u32[]{:S(2)}, u32[]{:S(2)}) %collective-permute-start.1) | collective-permute-done | bytes 262176 | tf_op jit(solution)/shard_map/ppermute | solution.py:21
  28.0 3.8 %collective-permute-start.2 = (bf16[4,128,256]{2,1,0:T(8,128)(2,1)S(1)}, bf16[4,128,256]{2,1,0:T(8,128)(2,1)S(1)}, u32[]{:S(2)}, u32[]{:S(2)}) collective-permute-start(bf16[4,128,256]{2,1,0:T(8,128)(2,1)S(1)} %pad_maximum_fusion.3), channel_id=1, source_target_pairs={{0,32},{8,40},{16,48},{24,56},{32,64},{40,72},{48,80},{56,88},{64,... | collective-permute-start | bytes 786440 | tf_op jit(solution)/shard_map/ppermute | solution.py:21
  31.8 0.2 and_reduce_fusion
  32.0 0.1 copy.25
  32.1 0.6 reshape.203.slot_ref
  32.7 0.6 reshape.209.use_ref
  33.3 0.1 copy.28
  33.4 0.6 reshape.210.early_ref
  34.0 4.3 %collective-permute-done.2 = bf16[4,128,256]{2,1,0:T(8,128)(2,1)S(1)} collective-permute-done((bf16[4,128,256]{2,1,0:T(8,128)(2,1)S(1)}, bf16[4,128,256]{2,1,0:T(8,128)(2,1)S(1)}, u32[]{:S(2)}, u32[]{:S(2)}) %collective-permute-start.2) | collective-permute-done | bytes 262176 | tf_op jit(solution)/shard_map/ppermute | solution.py:21
  38.4 0.0 collective-permute-done.3
  38.4 0.0 copy-start
  38.4 0.9 copy-done
  39.3 26.3 %shard_map.85 = (bf16[512,1024]{1,0:T(8,128)(2,1)}, f32[12,128,256]{2,1,0:T(8,128)}) custom-call(s32[16]{0:T(128)} %reshape.203.slot_ref, s32[16]{0:T(128)} %reshape.209.use_ref, s32[16]{0:T(128)} %reshape.210.early_ref, bf16[512,1024]{1,0:T(8,128)(2,1)} %q_ref.1, bf16[512,1024]{1,0:T(8,128)(2,1)} %g_ref.1, bf16[12,128,256]{2,1,0:T(8,128)(2,1)} %copy-done), custom_call_target="tpu_custom_call" | custom-call | tf_op jit(solution)/shard_map/pallas_call | solution.py:121
  65.5 1.5 %convert.5 = bf16[12,128,256]{2,1,0:T(8,128)(2,1)S(1)} convert(f32[12,128,256]{2,1,0:T(8,128)} %get-tuple-element.6) | non-fusion elementwise | flops 393216 | bytes 2359296 | tf_op jit(solution)/shard_map/convert.2
  67.1 1.9 %collective-permute-start.4 = (bf16[4,128,256]{2,1,0:T(8,128)(2,1)S(1)}, bf16[4,128,256]{2,1,0:T(8,128)(2,1)S(1)}, u32[]{:S(2)}, u32[]{:S(2)}) collective-permute-start(bf16[4,128,256]{2,1,0:T(8,128)(2,1)S(1)} %slice.153), channel_id=1, source_target_pairs={{32,0},{40,8},{48,16},{56,24},{64,32},{72,40},{80,48},{88,56},{96,... | collective-permute-start | bytes 786440 | tf_op jit(solution)/shard_map/ppermute | solution.py:21
  69.0 7.6 %collective-permute-done.4 = bf16[4,128,256]{2,1,0:T(8,128)(2,1)S(1)} collective-permute-done((bf16[4,128,256]{2,1,0:T(8,128)(2,1)S(1)}, bf16[4,128,256]{2,1,0:T(8,128)(2,1)S(1)}, u32[]{:S(2)}, u32[]{:S(2)}) %collective-permute-start.4) | collective-permute-done | bytes 262176 | tf_op jit(solution)/shard_map/ppermute | solution.py:21
  76.6 2.5 %collective-permute-start.5 = (bf16[4,128,256]{2,1,0:T(8,128)(2,1)S(1)}, bf16[4,128,256]{2,1,0:T(8,128)(2,1)S(1)}, u32[]{:S(2)}, u32[]{:S(2)}) collective-permute-start(bf16[4,128,256]{2,1,0:T(8,128)(2,1)S(1)} %pad_maximum_fusion.4), channel_id=1, source_target_pairs={{16,0},{24,8},{32,16},{40,24},{48,32},{56,40},{64,48},{72,56},{80,... | collective-permute-start | bytes 786440 | tf_op jit(solution)/shard_map/ppermute | solution.py:21
  79.2 7.6 %collective-permute-done.5 = bf16[4,128,256]{2,1,0:T(8,128)(2,1)S(1)} collective-permute-done((bf16[4,128,256]{2,1,0:T(8,128)(2,1)S(1)}, bf16[4,128,256]{2,1,0:T(8,128)(2,1)S(1)}, u32[]{:S(2)}, u32[]{:S(2)}) %collective-permute-start.5) | collective-permute-done | bytes 262176 | tf_op jit(solution)/shard_map/ppermute | solution.py:21
  86.8 1.9 %collective-permute-start.6 = (bf16[4,128,256]{2,1,0:T(8,128)(2,1)S(1)}, bf16[4,128,256]{2,1,0:T(8,128)(2,1)S(1)}, u32[]{:S(2)}, u32[]{:S(2)}) collective-permute-start(bf16[4,128,256]{2,1,0:T(8,128)(2,1)S(1)} %pad_maximum_fusion.5), channel_id=1, source_target_pairs={{8,0},{16,8},{24,16},{32,24},{40,32},{48,40},{56,48},{64,56},{72,6... | collective-permute-start | bytes 786440 | tf_op jit(solution)/shard_map/ppermute | solution.py:21
  88.8 2.1 %collective-permute-start.7 = (bf16[128,256]{1,0:T(8,128)(2,1)S(1)}, bf16[128,256]{1,0:T(8,128)(2,1)S(1)}, u32[]{:S(2)}, u32[]{:S(2)}) collective-permute-start(bf16[128,256]{1,0:T(8,128)(2,1)S(1)} %get-tuple-element.13), channel_id=1, source_target_pairs={{64,0},{72,8},{80,16},{88,24},{96,32},{104,40},{112,48},{120,56},{... | collective-permute-start | bytes 196616 | tf_op jit(solution)/shard_map/ppermute | solution.py:21
  90.9 2.8 %collective-permute-done.6 = bf16[4,128,256]{2,1,0:T(8,128)(2,1)S(1)} collective-permute-done((bf16[4,128,256]{2,1,0:T(8,128)(2,1)S(1)}, bf16[4,128,256]{2,1,0:T(8,128)(2,1)S(1)}, u32[]{:S(2)}, u32[]{:S(2)}) %collective-permute-start.6) | collective-permute-done | bytes 262176 | tf_op jit(solution)/shard_map/ppermute | solution.py:21
  93.9 6.8 %collective-permute-done.7 = bf16[128,256]{1,0:T(8,128)(2,1)S(1)} collective-permute-done((bf16[128,256]{1,0:T(8,128)(2,1)S(1)}, bf16[128,256]{1,0:T(8,128)(2,1)S(1)}, u32[]{:S(2)}, u32[]{:S(2)}) %collective-permute-start.7) | collective-permute-done | bytes 65568 | tf_op jit(solution)/shard_map/ppermute | solution.py:21
  100.6 0.1 convert_element_type.36
  100.7 0.0 copy-start.1
  100.7 0.4 multiply_reduce_fusion
  101.1 1.1 add_convert_fusion
  102.2 0.1 pad_maximum_fusion
  102.3 23.1 %all_to_all.16 = bf16[8,64,1280]{2,1,0:T(8,128)(2,1)S(1)} all-to-all(bf16[8,64,1280]{2,1,0:T(8,128)(2,1)S(1)} %bitcast.35), channel_id=1, replica_groups=mesh['ctx'=64,'head'=8] {'head'}, dimensions={0} | all-to-all | bytes 2621440 | tf_op jit(solution)/shard_map/all_to_all | solution.py:181
  125.4 0.1 slice_bitcast_fusion
  125.6 0.1 slice_bitcast_fusion.1
  125.6 1.1 copy.33
  126.7 0.7 copy.38
  127.4 0.7 copy.39
  (38 shorter events, 0.4 us)
Async XLA Ops:
  4.0 9.1 %copy-start.2 = (s32[256,4]{0,1:T(4,128)S(1)}, s32[256,4]{0,1:T(4,128)}, u32[]{:S(2)}) copy-start(s32[256,4]{0,1:T(4,128)} %param.10) | copy-start | bytes 12292
  4.7 10.1 %collective-permute-start = (bf16[4,128,256]{2,1,0:T(8,128)(2,1)S(1)}, bf16[4,128,256]{2,1,0:T(8,128)(2,1)S(1)}, u32[]{:S(2)}, u32[]{:S(2)}) collective-permute-start(bf16[4,128,256]{2,1,0:T(8,128)(2,1)S(1)} %gather_fusion.2), channel_id=1, source_target_pairs={{0,8},{8,16},{16,24},{24,32},{32,40},{40,48},{48,56},{56,64},{64,7... | collective-permute-start | bytes 786440 | tf_op jit(solution)/shard_map/ppermute | solution.py:21
  6.7 31.7 %collective-permute-start.3 = (bf16[128,256]{1,0:T(8,128)(2,1)S(1)}, bf16[128,256]{1,0:T(8,128)(2,1)S(1)}, u32[]{:S(2)}, u32[]{:S(2)}) collective-permute-start(bf16[128,256]{1,0:T(8,128)(2,1)S(1)} %get-tuple-element.15), channel_id=1, source_target_pairs={{0,64},{8,72},{16,80},{24,88},{32,96},{40,104},{48,112},{56,120},{... | collective-permute-start | bytes 196616 | tf_op jit(solution)/shard_map/ppermute | solution.py:21
  14.9 13.0 %collective-permute-start.1 = (bf16[4,128,256]{2,1,0:T(8,128)(2,1)S(1)}, bf16[4,128,256]{2,1,0:T(8,128)(2,1)S(1)}, u32[]{:S(2)}, u32[]{:S(2)}) collective-permute-start(bf16[4,128,256]{2,1,0:T(8,128)(2,1)S(1)} %pad_maximum_fusion.2), channel_id=1, source_target_pairs={{0,16},{8,24},{16,32},{24,40},{32,48},{40,56},{48,64},{56,72},{64,... | collective-permute-start | bytes 786440 | tf_op jit(solution)/shard_map/ppermute | solution.py:21
  28.0 10.4 %collective-permute-start.2 = (bf16[4,128,256]{2,1,0:T(8,128)(2,1)S(1)}, bf16[4,128,256]{2,1,0:T(8,128)(2,1)S(1)}, u32[]{:S(2)}, u32[]{:S(2)}) collective-permute-start(bf16[4,128,256]{2,1,0:T(8,128)(2,1)S(1)} %pad_maximum_fusion.3), channel_id=1, source_target_pairs={{0,32},{8,40},{16,48},{24,56},{32,64},{40,72},{48,80},{56,88},{64,... | collective-permute-start | bytes 786440 | tf_op jit(solution)/shard_map/ppermute | solution.py:21
  38.4 0.9 copy-start
  67.1 9.5 %collective-permute-start.4 = (bf16[4,128,256]{2,1,0:T(8,128)(2,1)S(1)}, bf16[4,128,256]{2,1,0:T(8,128)(2,1)S(1)}, u32[]{:S(2)}, u32[]{:S(2)}) collective-permute-start(bf16[4,128,256]{2,1,0:T(8,128)(2,1)S(1)} %slice.153), channel_id=1, source_target_pairs={{32,0},{40,8},{48,16},{56,24},{64,32},{72,40},{80,48},{88,56},{96,... | collective-permute-start | bytes 786440 | tf_op jit(solution)/shard_map/ppermute | solution.py:21
  76.6 10.2 %collective-permute-start.5 = (bf16[4,128,256]{2,1,0:T(8,128)(2,1)S(1)}, bf16[4,128,256]{2,1,0:T(8,128)(2,1)S(1)}, u32[]{:S(2)}, u32[]{:S(2)}) collective-permute-start(bf16[4,128,256]{2,1,0:T(8,128)(2,1)S(1)} %pad_maximum_fusion.4), channel_id=1, source_target_pairs={{16,0},{24,8},{32,16},{40,24},{48,32},{56,40},{64,48},{72,56},{80,... | collective-permute-start | bytes 786440 | tf_op jit(solution)/shard_map/ppermute | solution.py:21
  86.8 6.9 %collective-permute-start.6 = (bf16[4,128,256]{2,1,0:T(8,128)(2,1)S(1)}, bf16[4,128,256]{2,1,0:T(8,128)(2,1)S(1)}, u32[]{:S(2)}, u32[]{:S(2)}) collective-permute-start(bf16[4,128,256]{2,1,0:T(8,128)(2,1)S(1)} %pad_maximum_fusion.5), channel_id=1, source_target_pairs={{8,0},{16,8},{24,16},{32,24},{40,32},{48,40},{56,48},{64,56},{72,6... | collective-permute-start | bytes 786440 | tf_op jit(solution)/shard_map/ppermute | solution.py:21
  88.8 11.8 %collective-permute-start.7 = (bf16[128,256]{1,0:T(8,128)(2,1)S(1)}, bf16[128,256]{1,0:T(8,128)(2,1)S(1)}, u32[]{:S(2)}, u32[]{:S(2)}) collective-permute-start(bf16[128,256]{1,0:T(8,128)(2,1)S(1)} %get-tuple-element.13), channel_id=1, source_target_pairs={{64,0},{72,8},{80,16},{88,24},{96,32},{104,40},{112,48},{120,56},{... | collective-permute-start | bytes 196616 | tf_op jit(solution)/shard_map/ppermute | solution.py:21
  100.7 1.5 %copy-start.1 = (bf16[512,1024]{1,0:T(8,128)(2,1)S(1)}, bf16[512,1024]{1,0:T(8,128)(2,1)}, u32[]{:S(2)}) copy-start(bf16[512,1024]{1,0:T(8,128)(2,1)} %get-tuple-element.5) | copy-start | bytes 3145732

commit v3 on v2

--- a/solution.py
+++ b/solution.py
@@ -37,7 +37,7 @@
     return jnp.stack([step1[0], step2[0], step1[1], step4[0], step1[2], step2[2], step1[3], step8])
 
 
-def attn_kernel(slot_ref, use_ref, early_ref, q_ref, g_ref, kv_ref, dq_ref, acc_ref, kv_scr, dk_scr, dv_scr,
+def attn_kernel(slot_ref, use_ref, early_ref, q_ref, g_ref, kv_ref, dq_ref, acc_ref, kv_scr, qs_scr, gs_scr,
                 *, chosen, group, scaling):
     n = pl.program_id(0)
 
@@ -50,6 +50,11 @@
         kv_scr[e * BLOCK:(e + 1) * BLOCK, :] = kv_ref[slot_ref[n * chosen + e]]
     key_cat = kv_scr[:, :HEAD_DIM]
     value_cat = kv_scr[:, HEAD_DIM:]
+    for h in range(group):
+        qs_scr[h * BLOCK:(h + 1) * BLOCK, :] = q_ref[:, h * HEAD_DIM:(h + 1) * HEAD_DIM]
+        gs_scr[h * BLOCK:(h + 1) * BLOCK, :] = g_ref[:, h * HEAD_DIM:(h + 1) * HEAD_DIM]
+    q_all = qs_scr[...]
+    g_all = gs_scr[...]
 
     col = lax.broadcasted_iota(jnp.int32, (BLOCK, keys), 1)
     row = lax.broadcasted_iota(jnp.int32, (BLOCK, keys), 0)
@@ -62,36 +67,35 @@
         early_col = jnp.where(ent == e, early_ref[n * chosen + e], early_col)
     allowed = (use_col != 0) & ((early_col != 0) | (tok <= row))
 
-    dk_scr[...] = jnp.zeros_like(dk_scr)
-    dv_scr[...] = jnp.zeros_like(dv_scr)
     nt = (((1,), (1,)), ((), ()))
     tn = (((0,), (0,)), ((), ()))
+    rows = group * BLOCK
+    scores = lax.dot_general(q_all, key_cat, nt, preferred_element_type=jnp.float32) * scaling
+    scores = scores.reshape(group, BLOCK, keys)
+    scores = jnp.where(allowed[None], scores, -1e30)
+    row_max = jnp.max(scores, axis=2, keepdims=True)
+    total = jnp.sum(jnp.exp(scores - row_max), axis=2, keepdims=True)
+    log_total = row_max + jnp.log(total)
+    prob = jnp.exp(scores - log_total).reshape(rows, keys)
+    prob_half = prob.astype(jnp.bfloat16)
+    output = jnp.dot(prob_half, value_cat, preferred_element_type=jnp.float32)
+    output = output.astype(jnp.bfloat16).astype(jnp.float32)
+    row_dot = jnp.sum(g_all.astype(jnp.float32) * output, axis=1, keepdims=True)
+    prob_grad = lax.dot_general(g_all, value_cat, nt, preferred_element_type=jnp.float32)
+    score_grad = (prob * (prob_grad - row_dot) * scaling).astype(jnp.bfloat16)
+    dq_all = jnp.dot(score_grad, key_cat, preferred_element_type=jnp.float32).astype(jnp.bfloat16)
     for h in range(group):
-        cols = slice(h * HEAD_DIM, (h + 1) * HEAD_DIM)
-        q_h = q_ref[:, cols]
-        g_h = g_ref[:, cols]
-        scores = lax.dot_general(q_h, key_cat, nt, preferred_element_type=jnp.float32) * scaling
-        scores = jnp.where(allowed, scores, -1e30)
-        row_max = jnp.max(scores, axis=1, keepdims=True)
-        total = jnp.sum(jnp.exp(scores - row_max), axis=1, keepdims=True)
-        log_total = row_max + jnp.log(total)
-        prob = jnp.exp(scores - log_total)
-        prob_half = prob.astype(jnp.bfloat16)
-        output = jnp.dot(prob_half, value_cat, preferred_element_type=jnp.float32)
-        output = output.astype(jnp.bfloat16).astype(jnp.float32)
-        row_dot = jnp.sum(g_h.astype(jnp.float32) * output, axis=1, keepdims=True)
-        prob_grad = lax.dot_general(g_h, value_cat, nt, preferred_element_type=jnp.float32)
-        score_grad = (prob * (prob_grad - row_dot) * scaling).astype(jnp.bfloat16)
-        dq_h = jnp.dot(score_grad, key_cat, preferred_element_type=jnp.float32)
-        dq_ref[:, cols] = dq_h.astype(jnp.bfloat16)
-        dk_scr[...] += lax.dot_general(score_grad, q_h, tn, preferred_element_type=jnp.float32)
-        dv_scr[...] += lax.dot_general(prob_half, g_h, tn, preferred_element_type=jnp.float32)
+        dq_ref[:, h * HEAD_DIM:(h + 1) * HEAD_DIM] = dq_all[h * BLOCK:(h + 1) * BLOCK, :]
+    key_t = lax.dot_general(q_all, score_grad, tn, preferred_element_type=jnp.float32)
+    value_t = lax.dot_general(g_all, prob_half, tn, preferred_element_type=jnp.float32)
+    key_part = key_t.T
+    value_part = value_t.T
 
     for e in range(chosen):
         s = slot_ref[n * chosen + e]
-        rows = slice(e * BLOCK, (e + 1) * BLOCK)
-        acc_ref[s, :, :HEAD_DIM] += dk_scr[rows, :]
-        acc_ref[s, :, HEAD_DIM:] += dv_scr[rows, :]
+        part = slice(e * BLOCK, (e + 1) * BLOCK)
+        acc_ref[s, :, :HEAD_DIM] += key_part[part, :]
+        acc_ref[s, :, HEAD_DIM:] += value_part[part, :]
 
 
 def attention_terms(slots, usable, earlier, query_states, out_grad, kv_stock, chosen):
@@ -114,8 +118,8 @@
         ],
         scratch_shapes=[
             pltpu.VMEM((chosen * BLOCK, 2 * HEAD_DIM), jnp.bfloat16),
-            pltpu.VMEM((chosen * BLOCK, HEAD_DIM), jnp.float32),
-            pltpu.VMEM((chosen * BLOCK, HEAD_DIM), jnp.float32),
+            pltpu.VMEM((group * BLOCK, HEAD_DIM), jnp.bfloat16),
+            pltpu.VMEM((group * BLOCK, HEAD_DIM), jnp.bfloat16),
         ],
     )
     return pl.pallas_call(

time: 129 us -> 115 us (0.89)
  Pallas kernels: 26.3 us -> 12.8 us
    pallas_call x1, Pallas kernels: 26.3 us -> 12.8 us  [attention_terms(): pl.pallas_call(kernel, grid_spec=grid_spec, out_shape=[jax.ShapeDtypeStru...]
where the time goes in v3:
time: 115 us
  waiting for transfers between devices  39.4 us (34%)
  starting transfers between devices  24.8 us (22%)
  blocking collectives  23.1 us (20%)
  Pallas kernels  12.8 us (11%)
  local copies, waits for them, and re-layouts  8.4 us (7%)
  other arithmetic  4.99 us (4%)
    ppermute x8, waiting for transfers between devices, from_behind(): return lax.ppermute(x, axis, pairs)  39.4 us
    ppermute x8, starting transfers between devices, from_behind(): return lax.ppermute(x, axis, pairs)  24.8 us
    all_to_all x1, blocking collectives, body(): both = lax.all_to_all(both, 'head', split_axis=0, concat_axis=1, tiled=True)  23.1 us
    pallas_call x1, Pallas kernels, attention_terms(): pl.pallas_call(kernel, grid_spec=grid_spec, out_shape=[jax.ShapeDtypeStru...  12.8 us
  transfers between devices with their start and end apart: 8, of which 7 were waited for; matrix products, arithmetic and copies ran while one was open for 2% of the time, Pallas kernels for 0%

profile of v3, /device:TPU:192, one launch (start us, length us, event | category | flops | bytes accessed | tf_op | source)
XLA Modules:
  0.0 114.6 jit_solution(18416722032720306640)
XLA Ops:
  0.7 0.8 copy.29
  1.5 0.1 reshape.205
  1.6 0.6 gather_fusion
  2.2 0.2 fusion.2
  2.4 1.0 pad_maximum_fusion.1
  3.4 0.6 gather_fusion.1
  4.0 0.0 copy-start.2
  4.0 0.1 broadcast_select_fusion
  4.1 0.6 gather_fusion.2
  4.7 1.9 %collective-permute-start = (bf16[4,128,256]{2,1,0:T(8,128)(2,1)S(1)}, bf16[4,128,256]{2,1,0:T(8,128)(2,1)S(1)}, u32[]{:S(2)}, u32[]{:S(2)}) collective-permute-start(bf16[4,128,256]{2,1,0:T(8,128)(2,1)S(1)} %gather_fusion.2), channel_id=1, source_target_pairs={{0,8},{8,16},{16,24},{24,32},{32,40},{40,48},{48,56},{56,64},{64,7... | collective-permute-start | bytes 786440 | tf_op jit(solution)/shard_map/ppermute | solution.py:21
  6.7 6.4 %collective-permute-start.3 = (bf16[128,256]{1,0:T(8,128)(2,1)S(1)}, bf16[128,256]{1,0:T(8,128)(2,1)S(1)}, u32[]{:S(2)}, u32[]{:S(2)}) collective-permute-start(bf16[128,256]{1,0:T(8,128)(2,1)S(1)} %get-tuple-element.15), channel_id=1, source_target_pairs={{0,64},{8,72},{16,80},{24,88},{32,96},{40,104},{48,112},{56,120},{... | collective-permute-start | bytes 196616 | tf_op jit(solution)/shard_map/ppermute | solution.py:21
  13.1 0.1 compare_convert_fusion
  13.2 1.6 %collective-permute-done = bf16[4,128,256]{2,1,0:T(8,128)(2,1)S(1)} collective-permute-done((bf16[4,128,256]{2,1,0:T(8,128)(2,1)S(1)}, bf16[4,128,256]{2,1,0:T(8,128)(2,1)S(1)}, u32[]{:S(2)}, u32[]{:S(2)}) %collective-permute-start) | collective-permute-done | bytes 262176 | tf_op jit(solution)/shard_map/ppermute | solution.py:21
  14.9 4.2 %collective-permute-start.1 = (bf16[4,128,256]{2,1,0:T(8,128)(2,1)S(1)}, bf16[4,128,256]{2,1,0:T(8,128)(2,1)S(1)}, u32[]{:S(2)}, u32[]{:S(2)}) collective-permute-start(bf16[4,128,256]{2,1,0:T(8,128)(2,1)S(1)} %pad_maximum_fusion.2), channel_id=1, source_target_pairs={{0,16},{8,24},{16,32},{24,40},{32,48},{40,56},{48,64},{56,72},{64,... | collective-permute-start | bytes 786440 | tf_op jit(solution)/shard_map/ppermute | solution.py:21
  19.1 0.1 copy.26
  19.2 8.7 %collective-permute-done.1 = bf16[4,128,256]{2,1,0:T(8,128)(2,1)S(1)} collective-permute-done((bf16[4,128,256]{2,1,0:T(8,128)(2,1)S(1)}, bf16[4,128,256]{2,1,0:T(8,128)(2,1)S(1)}, u32[]{:S(2)}, u32[]{:S(2)}) %collective-permute-start.1) | collective-permute-done | bytes 262176 | tf_op jit(solution)/shard_map/ppermute | solution.py:21
  28.0 3.8 %collective-permute-start.2 = (bf16[4,128,256]{2,1,0:T(8,128)(2,1)S(1)}, bf16[4,128,256]{2,1,0:T(8,128)(2,1)S(1)}, u32[]{:S(2)}, u32[]{:S(2)}) collective-permute-start(bf16[4,128,256]{2,1,0:T(8,128)(2,1)S(1)} %pad_maximum_fusion.3), channel_id=1, source_target_pairs={{0,32},{8,40},{16,48},{24,56},{32,64},{40,72},{48,80},{56,88},{64,... | collective-permute-start | bytes 786440 | tf_op jit(solution)/shard_map/ppermute | solution.py:21
  31.8 0.2 and_reduce_fusion
  32.0 0.1 copy.25
  32.1 0.6 reshape.203.slot_ref
  32.7 0.6 reshape.209.use_ref
  33.3 0.1 copy.28
  33.4 0.6 reshape.210.early_ref
  34.0 4.3 %collective-permute-done.2 = bf16[4,128,256]{2,1,0:T(8,128)(2,1)S(1)} collective-permute-done((bf16[4,128,256]{2,1,0:T(8,128)(2,1)S(1)}, bf16[4,128,256]{2,1,0:T(8,128)(2,1)S(1)}, u32[]{:S(2)}, u32[]{:S(2)}) %collective-permute-start.2) | collective-permute-done | bytes 262176 | tf_op jit(solution)/shard_map/ppermute | solution.py:21
  38.4 0.0 collective-permute-done.3
  38.4 0.0 copy-start
  38.4 0.9 copy-done
  39.3 12.8 %shard_map.85 = (bf16[512,1024]{1,0:T(8,128)(2,1)}, f32[12,128,256]{2,1,0:T(8,128)}) custom-call(s32[16]{0:T(128)} %reshape.203.slot_ref, s32[16]{0:T(128)} %reshape.209.use_ref, s32[16]{0:T(128)} %reshape.210.early_ref, bf16[512,1024]{1,0:T(8,128)(2,1)} %q_ref.1, bf16[512,1024]{1,0:T(8,128)(2,1)} %g_ref.1, bf16[12,128,256]{2,1,0:T(8,128)(2,1)} %copy-done), custom_call_target="tpu_custom_call" | custom-call | tf_op jit(solution)/shard_map/pallas_call | solution.py:125
  52.1 1.5 %convert.5 = bf16[12,128,256]{2,1,0:T(8,128)(2,1)S(1)} convert(f32[12,128,256]{2,1,0:T(8,128)} %get-tuple-element.6) | non-fusion elementwise | flops 393216 | bytes 2359296 | tf_op jit(solution)/shard_map/convert.2
  53.6 1.9 %collective-permute-start.4 = (bf16[4,128,256]{2,1,0:T(8,128)(2,1)S(1)}, bf16[4,128,256]{2,1,0:T(8,128)(2,1)S(1)}, u32[]{:S(2)}, u32[]{:S(2)}) collective-permute-start(bf16[4,128,256]{2,1,0:T(8,128)(2,1)S(1)} %slice.153), channel_id=1, source_target_pairs={{32,0},{40,8},{48,16},{56,24},{64,32},{72,40},{80,48},{88,56},{96,... | collective-permute-start | bytes 786440 | tf_op jit(solution)/shard_map/ppermute | solution.py:21
  55.6 7.6 %collective-permute-done.4 = bf16[4,128,256]{2,1,0:T(8,128)(2,1)S(1)} collective-permute-done((bf16[4,128,256]{2,1,0:T(8,128)(2,1)S(1)}, bf16[4,128,256]{2,1,0:T(8,128)(2,1)S(1)}, u32[]{:S(2)}, u32[]{:S(2)}) %collective-permute-start.4) | collective-permute-done | bytes 262176 | tf_op jit(solution)/shard_map/ppermute | solution.py:21
  63.2 2.5 %collective-permute-start.5 = (bf16[4,128,256]{2,1,0:T(8,128)(2,1)S(1)}, bf16[4,128,256]{2,1,0:T(8,128)(2,1)S(1)}, u32[]{:S(2)}, u32[]{:S(2)}) collective-permute-start(bf16[4,128,256]{2,1,0:T(8,128)(2,1)S(1)} %pad_maximum_fusion.4), channel_id=1, source_target_pairs={{16,0},{24,8},{32,16},{40,24},{48,32},{56,40},{64,48},{72,56},{80,... | collective-permute-start | bytes 786440 | tf_op jit(solution)/shard_map/ppermute | solution.py:21
  65.7 7.6 %collective-permute-done.5 = bf16[4,128,256]{2,1,0:T(8,128)(2,1)S(1)} collective-permute-done((bf16[4,128,256]{2,1,0:T(8,128)(2,1)S(1)}, bf16[4,128,256]{2,1,0:T(8,128)(2,1)S(1)}, u32[]{:S(2)}, u32[]{:S(2)}) %collective-permute-start.5) | collective-permute-done | bytes 262176 | tf_op jit(solution)/shard_map/ppermute | solution.py:21
  73.4 1.9 %collective-permute-start.6 = (bf16[4,128,256]{2,1,0:T(8,128)(2,1)S(1)}, bf16[4,128,256]{2,1,0:T(8,128)(2,1)S(1)}, u32[]{:S(2)}, u32[]{:S(2)}) collective-permute-start(bf16[4,128,256]{2,1,0:T(8,128)(2,1)S(1)} %pad_maximum_fusion.5), channel_id=1, source_target_pairs={{8,0},{16,8},{24,16},{32,24},{40,32},{48,40},{56,48},{64,56},{72,6... | collective-permute-start | bytes 786440 | tf_op jit(solution)/shard_map/ppermute | solution.py:21
  75.3 2.1 %collective-permute-start.7 = (bf16[128,256]{1,0:T(8,128)(2,1)S(1)}, bf16[128,256]{1,0:T(8,128)(2,1)S(1)}, u32[]{:S(2)}, u32[]{:S(2)}) collective-permute-start(bf16[128,256]{1,0:T(8,128)(2,1)S(1)} %get-tuple-element.13), channel_id=1, source_target_pairs={{64,0},{72,8},{80,16},{88,24},{96,32},{104,40},{112,48},{120,56},{... | collective-permute-start | bytes 196616 | tf_op jit(solution)/shard_map/ppermute | solution.py:21
  77.5 2.9 %collective-permute-done.6 = bf16[4,128,256]{2,1,0:T(8,128)(2,1)S(1)} collective-permute-done((bf16[4,128,256]{2,1,0:T(8,128)(2,1)S(1)}, bf16[4,128,256]{2,1,0:T(8,128)(2,1)S(1)}, u32[]{:S(2)}, u32[]{:S(2)}) %collective-permute-start.6) | collective-permute-done | bytes 262176 | tf_op jit(solution)/shard_map/ppermute | solution.py:21
  80.4 6.8 %collective-permute-done.7 = bf16[128,256]{1,0:T(8,128)(2,1)S(1)} collective-permute-done((bf16[128,256]{1,0:T(8,128)(2,1)S(1)}, bf16[128,256]{1,0:T(8,128)(2,1)S(1)}, u32[]{:S(2)}, u32[]{:S(2)}) %collective-permute-start.7) | collective-permute-done | bytes 65568 | tf_op jit(solution)/shard_map/ppermute | solution.py:21
  87.2 0.1 convert_element_type.36
  87.3 0.0 copy-start.1
  87.3 0.4 multiply_reduce_fusion
  87.6 1.1 add_convert_fusion
  88.8 0.1 pad_maximum_fusion
  88.9 23.1 %all_to_all.16 = bf16[8,64,1280]{2,1,0:T(8,128)(2,1)S(1)} all-to-all(bf16[8,64,1280]{2,1,0:T(8,128)(2,1)S(1)} %bitcast.35), channel_id=1, replica_groups=mesh['ctx'=64,'head'=8] {'head'}, dimensions={0} | all-to-all | bytes 2621440 | tf_op jit(solution)/shard_map/all_to_all | solution.py:185
  112.0 0.1 slice_bitcast_fusion
  112.1 0.1 slice_bitcast_fusion.1
  112.2 1.1 copy.33
  113.3 0.7 copy.38
  113.9 0.7 copy.39
  (38 shorter events, 0.4 us)
Async XLA Ops:
  4.0 9.1 %copy-start.2 = (s32[256,4]{0,1:T(4,128)S(1)}, s32[256,4]{0,1:T(4,128)}, u32[]{:S(2)}) copy-start(s32[256,4]{0,1:T(4,128)} %param.10) | copy-start | bytes 12292
  4.7 10.1 %collective-permute-start = (bf16[4,128,256]{2,1,0:T(8,128)(2,1)S(1)}, bf16[4,128,256]{2,1,0:T(8,128)(2,1)S(1)}, u32[]{:S(2)}, u32[]{:S(2)}) collective-permute-start(bf16[4,128,256]{2,1,0:T(8,128)(2,1)S(1)} %gather_fusion.2), channel_id=1, source_target_pairs={{0,8},{8,16},{16,24},{24,32},{32,40},{40,48},{48,56},{56,64},{64,7... | collective-permute-start | bytes 786440 | tf_op jit(solution)/shard_map/ppermute | solution.py:21
  6.7 31.7 %collective-permute-start.3 = (bf16[128,256]{1,0:T(8,128)(2,1)S(1)}, bf16[128,256]{1,0:T(8,128)(2,1)S(1)}, u32[]{:S(2)}, u32[]{:S(2)}) collective-permute-start(bf16[128,256]{1,0:T(8,128)(2,1)S(1)} %get-tuple-element.15), channel_id=1, source_target_pairs={{0,64},{8,72},{16,80},{24,88},{32,96},{40,104},{48,112},{56,120},{... | collective-permute-start | bytes 196616 | tf_op jit(solution)/shard_map/ppermute | solution.py:21
  14.9 13.0 %collective-permute-start.1 = (bf16[4,128,256]{2,1,0:T(8,128)(2,1)S(1)}, bf16[4,128,256]{2,1,0:T(8,128)(2,1)S(1)}, u32[]{:S(2)}, u32[]{:S(2)}) collective-permute-start(bf16[4,128,256]{2,1,0:T(8,128)(2,1)S(1)} %pad_maximum_fusion.2), channel_id=1, source_target_pairs={{0,16},{8,24},{16,32},{24,40},{32,48},{40,56},{48,64},{56,72},{64,... | collective-permute-start | bytes 786440 | tf_op jit(solution)/shard_map/ppermute | solution.py:21
  28.0 10.4 %collective-permute-start.2 = (bf16[4,128,256]{2,1,0:T(8,128)(2,1)S(1)}, bf16[4,128,256]{2,1,0:T(8,128)(2,1)S(1)}, u32[]{:S(2)}, u32[]{:S(2)}) collective-permute-start(bf16[4,128,256]{2,1,0:T(8,128)(2,1)S(1)} %pad_maximum_fusion.3), channel_id=1, source_target_pairs={{0,32},{8,40},{16,48},{24,56},{32,64},{40,72},{48,80},{56,88},{64,... | collective-permute-start | bytes 786440 | tf_op jit(solution)/shard_map/ppermute | solution.py:21
  38.4 0.9 copy-start
  53.6 9.5 %collective-permute-start.4 = (bf16[4,128,256]{2,1,0:T(8,128)(2,1)S(1)}, bf16[4,128,256]{2,1,0:T(8,128)(2,1)S(1)}, u32[]{:S(2)}, u32[]{:S(2)}) collective-permute-start(bf16[4,128,256]{2,1,0:T(8,128)(2,1)S(1)} %slice.153), channel_id=1, source_target_pairs={{32,0},{40,8},{48,16},{56,24},{64,32},{72,40},{80,48},{88,56},{96,... | collective-permute-start | bytes 786440 | tf_op jit(solution)/shard_map/ppermute | solution.py:21
  63.2 10.2 %collective-permute-start.5 = (bf16[4,128,256]{2,1,0:T(8,128)(2,1)S(1)}, bf16[4,128,256]{2,1,0:T(8,128)(2,1)S(1)}, u32[]{:S(2)}, u32[]{:S(2)}) collective-permute-start(bf16[4,128,256]{2,1,0:T(8,128)(2,1)S(1)} %pad_maximum_fusion.4), channel_id=1, source_target_pairs={{16,0},{24,8},{32,16},{40,24},{48,32},{56,40},{64,48},{72,56},{80,... | collective-permute-start | bytes 786440 | tf_op jit(solution)/shard_map/ppermute | solution.py:21
  73.4 6.9 %collective-permute-start.6 = (bf16[4,128,256]{2,1,0:T(8,128)(2,1)S(1)}, bf16[4,128,256]{2,1,0:T(8,128)(2,1)S(1)}, u32[]{:S(2)}, u32[]{:S(2)}) collective-permute-start(bf16[4,128,256]{2,1,0:T(8,128)(2,1)S(1)} %pad_maximum_fusion.5), channel_id=1, source_target_pairs={{8,0},{16,8},{24,16},{32,24},{40,32},{48,40},{56,48},{64,56},{72,6... | collective-permute-start | bytes 786440 | tf_op jit(solution)/shard_map/ppermute | solution.py:21
  75.3 11.8 %collective-permute-start.7 = (bf16[128,256]{1,0:T(8,128)(2,1)S(1)}, bf16[128,256]{1,0:T(8,128)(2,1)S(1)}, u32[]{:S(2)}, u32[]{:S(2)}) collective-permute-start(bf16[128,256]{1,0:T(8,128)(2,1)S(1)} %get-tuple-element.13), channel_id=1, source_target_pairs={{64,0},{72,8},{80,16},{88,24},{96,32},{104,40},{112,48},{120,56},{... | collective-permute-start | bytes 196616 | tf_op jit(solution)/shard_map/ppermute | solution.py:21
  87.3 1.5 %copy-start.1 = (bf16[512,1024]{1,0:T(8,128)(2,1)S(1)}, bf16[512,1024]{1,0:T(8,128)(2,1)}, u32[]{:S(2)}) copy-start(bf16[512,1024]{1,0:T(8,128)(2,1)} %get-tuple-element.5) | copy-start | bytes 3145732
